TPU v7x, 512 devices: a whole 4x4x16 slice. The times are simulated.
512 devices in a mesh: dp: 32 (over y_hi, z), tensor: 16 (over x, y_lo, core).
Axes of the slice: x: 4, y: 4 (y_hi: 2, y_lo: 2; y = y_hi * 2 + y_lo), z: 16, core: 2. Of those that a mesh axis runs over, the one named last changes fastest.
Arguments:
- residual: bfloat16 [65536, 2048], P(('dp', 'tensor')), may hold values from -0.59765625 to 0.59765625
- queries: bfloat16 [65536, 2048], P(('dp', 'tensor')), may hold values from -27 to 27
- new_keys: bfloat16 [65536, 2048], P(('dp', 'tensor')), may hold values from -27 to 27
- new_values: bfloat16 [65536, 2048], P(('dp', 'tensor')), may hold values from -6 to 6
- lengths: int32 [32, 2], P('dp'), may hold values from 1 to 1536, 2048 in all within a row
- page_order: int32 [32, 17], P('dp'), may hold values from 0 to 16, each once within a row
- wo_shard: float32 [2048, 2048], P('tensor', 'dp'), may hold values from -0.125 to 0.125
- norm_gain: float32 [2048], replicated, may hold values from 0.1 to 1.9
- gate_shard: float32 [16, 2048, 256], P('tensor', 'dp'), may hold values from -0.125 to 0.125
- up_shard: float32 [16, 2048, 256], P('tensor', 'dp'), may hold values from -0.125 to 0.125
- down_shard: float32 [16, 256, 2048], P('tensor', None, 'dp'), may hold values from -0.1875 to 0.1875
- routes: int32 [65536, 8], P(('dp', 'tensor')), may hold values from 0 to 63, as said below
- route_weights: float32 [65536, 8], P(('dp', 'tensor')), may hold values from 0.05 to 0.3
Outputs:
- hidden_mid: bfloat16 [65536, 2048], P(('dp', 'tensor'))
- expert_sum: bfloat16 [65536, 2048], P(('dp', 'tensor'))
- key_pages: bfloat16 [544, 128, 2048], P('dp', None, 'tensor')
- value_pages: bfloat16 [544, 128, 2048], P('dp', None, 'tensor')
Inputs may be any that keep to these rules, and one draw needn't show every extreme that they name: `routes`: each row names 8 different experts. Within each aligned block of 128 rows (the rows of one device), each expert below 4 is named by 1 to 16 rows; one of them, the same in all blocks of a draw, by exactly 16 rows in every block, the others by at most 8 rows.
All inputs are finite; a program needn't handle non-finite values.
Results may differ from a plain program's by a relative error of at most 0.015.
Values may be sent and summed in bfloat16 or wider, within the bound.
No kernel may reach another device: no remote copies, remote signals or barrier semaphores. Data moves between devices by JAX's collectives and lax.ppermute only.
A program may use at most 64 MiB of HBM per device.

v0:
```python
import math

import jax
import jax.numpy as jnp
from jax import lax
from jax.sharding import PartitionSpec as P

D = 2048
HEADS = 16
HD = 128
SPLIT = 4
PAGE = 128
MOST = 16


def page_layout(lens_row, order_row, group_rows, pool_size):
    index_rows = jnp.arange(group_rows, dtype=jnp.int32)
    prompt_ends = jnp.cumsum(lens_row)
    segment = jnp.sum((index_rows[:, None] >= prompt_ends[None, :]).astype(jnp.int32), axis=1)
    prompt_starts = prompt_ends - lens_row
    owner_mask = (
        segment[:, None] == jnp.arange(lens_row.shape[0], dtype=jnp.int32)[None, :]
    ).astype(jnp.int32)
    begins = jnp.sum(owner_mask * prompt_starts[None, :], axis=1)
    page_count = (lens_row + PAGE - 1) // PAGE
    first_page = jnp.cumsum(page_count) - page_count
    page_first = jnp.sum(owner_mask * first_page[None, :], axis=1)
    position = index_rows - begins
    logical = page_first + position // PAGE
    matched = (logical[:, None] == jnp.arange(pool_size, dtype=jnp.int32)[None, :]).astype(
        jnp.int32
    )
    physical = jnp.sum(matched * order_row[None, :], axis=1)
    return (segment, physical * PAGE + position % PAGE)


def attend_group(q_heads, k_heads, v_heads, segment, heads_here):
    group_rows = q_heads.shape[0]
    block_rows = min(512, group_rows)
    count_blocks = group_rows // block_rows
    q_blocks = q_heads.reshape(count_blocks, block_rows, heads_here, HD)
    seg_blocks = segment.reshape(count_blocks, block_rows)
    k_split = k_heads.reshape(group_rows, heads_here, HD)
    v_split = v_heads.reshape(group_rows, heads_here, HD)

    def one_block(block_pair):
        q_block, seg_block = block_pair
        scores = jnp.einsum(
            "qhd,khd->hqk", q_block, k_split, preferred_element_type=jnp.float32
        ) / math.sqrt(HD)
        same_prompt = seg_block[:, None] == segment[None, :]
        scores = jnp.where(same_prompt[None, :, :], scores, -jnp.inf)
        row_max = jnp.max(scores, axis=2, keepdims=True)
        weights = jnp.exp(scores - row_max)
        totals = jnp.sum(weights, axis=2)
        output = jnp.einsum(
            "hqk,khd->qhd",
            weights.astype(jnp.bfloat16),
            v_split,
            preferred_element_type=jnp.float32,
        )
        output = output / jnp.transpose(totals)[:, :, None]
        return output.astype(jnp.bfloat16).reshape(block_rows, heads_here * HD)

    return lax.map(one_block, (q_blocks, seg_blocks)).reshape(group_rows, heads_here * HD)


def body(
    residual,
    queries,
    new_keys,
    new_values,
    lengths,
    page_order,
    wo_shard,
    norm_gain,
    gate_shard,
    up_shard,
    down_shard,
    routes,
    route_weights,
):
    tensor_count = lax.axis_size("tensor")
    heads_here = HEADS // tensor_count
    q_heads, k_heads, v_heads = (
        lax.all_to_all(queries, "tensor", split_axis=1, concat_axis=0, tiled=True),
        lax.all_to_all(new_keys, "tensor", split_axis=1, concat_axis=0, tiled=True),
        lax.all_to_all(new_values, "tensor", split_axis=1, concat_axis=0, tiled=True),
    )
    group_rows = q_heads.shape[0]
    pool_size = page_order.shape[1]
    segment, slot_index = page_layout(lengths[0], page_order[0], group_rows, pool_size)
    head_width = k_heads.shape[1]
    key_pages = (
        jnp.zeros((pool_size * PAGE, head_width), jnp.bfloat16)
        .at[slot_index]
        .set(k_heads)
        .reshape(pool_size, PAGE, head_width)
    )
    value_pages = (
        jnp.zeros((pool_size * PAGE, head_width), jnp.bfloat16)
        .at[slot_index]
        .set(v_heads)
        .reshape(pool_size, PAGE, head_width)
    )
    attended = attend_group(q_heads, k_heads, v_heads, segment, heads_here)
    token_rows = lax.all_to_all(attended, "tensor", split_axis=0, concat_axis=1, tiled=True)
    wo_cast = wo_shard.astype(jnp.bfloat16)
    columns = lax.all_gather(wo_cast, "dp", axis=1, tiled=True)
    projected = jnp.dot(
        token_rows,
        lax.all_gather(columns, "tensor", axis=0, tiled=True),
        preferred_element_type=jnp.float32,
    )
    hidden_mid = (residual.astype(jnp.float32) + projected).astype(jnp.bfloat16)
    mid_float = hidden_mid.astype(jnp.float32)
    normed = (
        mid_float
        * lax.rsqrt(jnp.mean(mid_float * mid_float, axis=1, keepdims=True) + 1e-06)
        * norm_gain
    ).astype(jnp.bfloat16)
    flight = tensor_count // SPLIT
    flight_ids = jnp.arange(flight, dtype=jnp.int32)
    named_here = routes[:, :, None] == flight_ids[None, None, :]
    routed = jnp.any(named_here, axis=1)
    weight_sum = jnp.sum(jnp.where(named_here, route_weights[:, :, None], 0.0), axis=1)
    ranked = jnp.cumsum(routed.astype(jnp.int32), axis=0) - 1
    picked = (ranked[:, :, None] == jnp.arange(MOST, dtype=jnp.int32)[None, None, :]) & routed[
        :, :, None
    ]
    outgoing = jnp.einsum(
        "tem,td->emd", picked.astype(jnp.bfloat16), normed, preferred_element_type=jnp.float32
    ).astype(jnp.bfloat16)
    outgoing = jnp.repeat(outgoing, SPLIT, axis=0)
    gate_full, up_full, down_full = (
        lax.all_gather(gate_shard.astype(jnp.bfloat16), "dp", axis=1, tiled=True),
        lax.all_gather(up_shard.astype(jnp.bfloat16), "dp", axis=1, tiled=True),
        lax.all_gather(down_shard.astype(jnp.bfloat16), "dp", axis=2, tiled=True),
    )
    arrived = lax.all_to_all(outgoing, "tensor", split_axis=0, concat_axis=0, tiled=True)
    gate_val = jnp.einsum("smd,dp->smp", arrived, gate_full[0], preferred_element_type=jnp.float32)
    up_val = jnp.einsum("smd,dp->smp", arrived, up_full[0], preferred_element_type=jnp.float32)
    inner_act = (jax.nn.silu(gate_val) * up_val).astype(jnp.bfloat16)
    result = jnp.einsum(
        "smp,pd->smd", inner_act, down_full[0], preferred_element_type=jnp.float32
    ).astype(jnp.bfloat16)
    returned = lax.all_to_all(result, "tensor", split_axis=0, concat_axis=0, tiled=True)
    summed = jnp.sum(returned.reshape(flight, SPLIT, MOST, D).astype(jnp.float32), axis=1)
    mixing = picked.astype(jnp.float32) * weight_sum[:, :, None]
    expert_sum = jnp.einsum("tem,emd->td", mixing, summed, precision=lax.Precision.HIGHEST).astype(
        jnp.bfloat16
    )
    return (hidden_mid, expert_sum, key_pages, value_pages)


def solution(mesh):
    return jax.shard_map(
        body,
        mesh=mesh,
        in_specs=(
            P(("dp", "tensor"), None),
            P(("dp", "tensor"), None),
            P(("dp", "tensor"), None),
            P(("dp", "tensor"), None),
            P("dp", None),
            P("dp", None),
            P("tensor", "dp"),
            P(),
            P("tensor", "dp", None),
            P("tensor", "dp", None),
            P("tensor", None, "dp"),
            P(("dp", "tensor"), None),
            P(("dp", "tensor"), None),
        ),
        out_specs=(
            P(("dp", "tensor"), None),
            P(("dp", "tensor"), None),
            P("dp", None, "tensor"),
            P("dp", None, "tensor"),
        ),
        check_vma=False,
    )
```

profile of v0, /device:TPU:1, one launch (start us, length us, event | category | flops | bytes accessed | tf_op | source)
XLA Modules:
  0.0 635.9 jit_solution(6192346306838084614)
XLA Ops:
  8.1 77.1 %all_gather.15 = bf16[128,2048]{0,1:T(8,128)(2,1)} all-gather(bf16[128,64]{0,1:T(8,128)(2,1)S(1)} %convert_element_type.68), channel_id=1, replica_groups=mesh['dp'=32,'tensor'=16] {'dp'}, dimensions={1}, use_global_device_ids=true | all-gather | bytes 540672 | tf_op jit(solution)/shard_map/all_gather | solution.py:109
  86.7 2.0 copy.76
  88.7 19.2 %all-to-all-start.1 = ((bf16[128,16,128]{0,2,1:T(8,128)(2,1)}), bf16[128,16,128]{0,2,1:T(8,128)(2,1)S(1)}, u32[]{:S(2)}, u32[]{:S(2)}) async-start(bf16[128,16,128]{0,2,1:T(8,128)(2,1)} %bitcast.14), calls=%async_computation.1 | async-start | bytes 1048576 | tf_op jit(solution)/shard_map/all_to_all | solution.py:87
  107.9 2.0 copy.78
  109.9 9.6 %all-to-all-done.1 = bf16[128,16,128]{0,2,1:T(8,128)(2,1)S(1)} async-done(((bf16[128,16,128]{0,2,1:T(8,128)(2,1)}), bf16[128,16,128]{0,2,1:T(8,128)(2,1)S(1)}, u32[]{:S(2)}, u32[]{:S(2)}) %all-to-all-start.1) | async-done | bytes 524320 | tf_op jit(solution)/shard_map/all_to_all | solution.py:87
  119.5 4.6 all-to-all-start.2
  125.1 12.6 %all-to-all-done.2 = bf16[128,16,128]{0,2,1:T(8,128)(2,1)S(1)} async-done(((bf16[128,16,128]{0,2,1:T(8,128)(2,1)}), bf16[128,16,128]{0,2,1:T(8,128)(2,1)S(1)}, u32[]{:S(2)}, u32[]{:S(2)}) %all-to-all-start.2) | async-done | bytes 524320 | tf_op jit(solution)/shard_map/all_to_all | solution.py:88
  137.8 5.7 all-to-all-start
  145.1 11.8 %all-to-all-done = bf16[128,16,128]{0,2,1:T(8,128)(2,1)S(1)} async-done(((bf16[128,16,128]{0,2,1:T(8,128)(2,1)}), bf16[128,16,128]{0,2,1:T(8,128)(2,1)S(1)}, u32[]{:S(2)}, u32[]{:S(2)}) %all-to-all-start) | async-done | bytes 524320 | tf_op jit(solution)/shard_map/all_to_all | solution.py:86
  157.2 12.3 %while.10 = (s32[]{:T(128)}, bf16[4,512,128]{2,1,0:T(8,128)(2,1)}, s32[4,512]{1,0:T(4,128)S(1)}, s32[2048]{0:T(1024)S(1)}, bf16[4,512,1,128]{3,1,2,0:T(8,128)(2,...) while((s32[]{:T(128)}, bf16[4,512,128]{2,1,0:T(8,128)(2,1)}, ...), condition=%wide.region_5.6_spmd, body=%wide.region_2.0_spmd.sunk | while | flops 545389568 | bytes 13918813 | solution.py:65
  169.5 4.9 all-to-all-start.3
  175.5 8.6 %all-to-all-done.3 = bf16[16,128,128]{2,1,0:T(8,128)(2,1)S(1)} async-done(((bf16[16,128,128]{2,1,0:T(8,128)(2,1)}), bf16[16,128,128]{2,1,0:T(8,128)(2,1)S(1)}, u32[]{:S(2)}, u32[]{:S(2)}) %all-to-all-start.3) | async-done | bytes 524320 | tf_op jit(solution)/shard_map/all_to_all | solution.py:107
  184.4 6.4 %fusion.28 = (f32[128]{0:T(128)S(1)}, bf16[128,2048]{1,0:T(8,128)(2,1)S(1)}) fusion(bf16[128,2048]{0,1:T(8,128)(2,1)S(1)} %bitcast.108, bf16[2048,2048]{0,1:T(8,128)(2,1)} %all-gather.5.cloned.1.call-done, bf16[128,2048]{1,0:T(8,128)(2,1)S(1)} %copy-done), kind=kOutput, calls=%fused_computation.30 | convolution fusion | flops 1075314560 | bytes 9961984 | tf_op jit(solution)/shard_map/dot_general | solution.py:110
  192.3 4.7 all-to-all-start.4
  197.3 114.6 %all-gather.7.cloned.1.call-done = bf16[1,2048,256]{2,1,0:T(8,128)(2,1)} async-done(((bf16[1,64,256]{2,1,0:T(8,128)(2,1)}), bf16[1,2048,256]{2,1,0:T(8,128)(2,1)}) %all-gather.7.cloned.1.call-update) | async-done | bytes 1048592 | tf_op jit(solution)/shard_map/all_gather | solution.py:136
  311.9 1.7 fusion.34
  313.6 139.5 %all-gather.11.cloned.1.call-done = bf16[1,256,2048]{1,2,0:T(8,128)(2,1)} async-done(((bf16[1,256,64]{1,2,0:T(8,128)(2,1)}), bf16[1,256,2048]{1,2,0:T(8,128)(2,1)}) %all-gather.11.cloned.1.call-update) | async-done | bytes 1048592 | tf_op jit(solution)/shard_map/all_gather | solution.py:138
  453.0 141.0 %all-gather.9.cloned.1.call-done = bf16[1,2048,256]{2,1,0:T(8,128)(2,1)} async-done(((bf16[1,64,256]{2,1,0:T(8,128)(2,1)}), bf16[1,2048,256]{2,1,0:T(8,128)(2,1)}) %all-gather.9.cloned.1.call-update) | async-done | bytes 1048592 | tf_op jit(solution)/shard_map/all_gather | solution.py:137
  594.0 3.8 convolution_convert_fusion
  597.8 14.0 %all-to-all-start.5 = ((bf16[16,16,2048]{2,1,0:T(8,128)(2,1)}), bf16[16,16,2048]{2,1,0:T(8,128)(2,1)S(1)}, u32[]{:S(2)}, u32[]{:S(2)}) async-start(bf16[16,16,2048]{2,1,0:T(8,128)(2,1)} %convolution_convert_fusion), calls=%async_computation.5 | async-start | bytes 2097152 | tf_op jit(solution)/shard_map/all_to_all | solution.py:147
  612.1 6.5 %scatter_custom_fusion = bf16[2176,128]{1,0:T(8,128)(2,1)} fusion(s32[2048]{0:T(1024)S(1)} %bitcast.121, bf16[2048,128]{1,0:T(8,128)(2,1)S(1)} %bitcast.116, bf16[]{:T(256)} %constant.81.clone.1), kind=kCustom, calls=%fused_computation.42 | custom fusion | bytes 557058 | tf_op jit(solution)/shard_map/scatter | solution.py:97
  618.6 6.5 %scatter_custom_fusion.1 = bf16[2176,128]{1,0:T(8,128)(2,1)} fusion(s32[2048]{0:T(1024)S(1)} %bitcast.122, bf16[2048,128]{1,0:T(8,128)(2,1)S(1)} %bitcast.107, bf16[]{:T(256)} %constant.81.clone.1), kind=kCustom, calls=%fused_computation.40 | custom fusion | bytes 557058 | tf_op jit(solution)/shard_map/scatter | solution.py:103
  625.2 2.2 all-to-all-done.5
  627.5 1.8 fusion.26
  (78 shorter events, 21.0 us)
Async XLA Ops:
  7.2 116.9 %copy-start.2 = (bf16[128,2048]{1,0:T(8,128)(2,1)S(1)}, bf16[128,2048]{1,0:T(8,128)(2,1)}, u32[]{:S(2)}) copy-start(bf16[128,2048]{1,0:T(8,128)(2,1)} %param.16) | copy-start | bytes 1572868
  7.2 136.3 %copy-start.3 = (f32[1,256,64]{1,2,0:T(8,128)S(1)}, f32[1,256,64]{1,2,0:T(8,128)}, u32[]{:S(2)}) copy-start(f32[1,256,64]{1,2,0:T(8,128)} %param.25) | copy-start | bytes 196612
  7.2 137.0 %copy-start.8 = (s32[1,2]{1,0:T(1,128)S(1)}, s32[1,2]{1,0:T(1,128)}, u32[]{:S(2)}) copy-start(s32[1,2]{1,0:T(1,128)} %param.19) | copy-start | bytes 28
  7.2 177.2 %all-gather.5.cloned.1.call-start = ((), (), s32[]{:S(2)}) async-start(), calls=%async_computation.6 | async-start | bytes 8912896 | tf_op jit(solution)/shard_map/all_gather | solution.py:112
  85.2 226.8 %all-gather.7.cloned.1.call-start = ((), (), s32[]{:S(2)}) async-start(), calls=%async_computation.7 | async-start | bytes 1081344 | tf_op jit(solution)/shard_map/all_gather | solution.py:136
  88.7 30.8 %all-to-all-start.1 = ((bf16[128,16,128]{0,2,1:T(8,128)(2,1)}), bf16[128,16,128]{0,2,1:T(8,128)(2,1)S(1)}, u32[]{:S(2)}, u32[]{:S(2)}) async-start(bf16[128,16,128]{0,2,1:T(8,128)(2,1)} %bitcast.14), calls=%async_computation.1 | async-start | bytes 1048576 | tf_op jit(solution)/shard_map/all_to_all | solution.py:87
  119.5 18.2 %all-to-all-start.2 = ((bf16[128,16,128]{0,2,1:T(8,128)(2,1)}), bf16[128,16,128]{0,2,1:T(8,128)(2,1)S(1)}, u32[]{:S(2)}, u32[]{:S(2)}) async-start(bf16[128,16,128]{0,2,1:T(8,128)(2,1)} %bitcast.17), calls=%async_computation.2 | async-start | bytes 1048576 | tf_op jit(solution)/shard_map/all_to_all | solution.py:88
  137.8 19.1 %all-to-all-start = ((bf16[128,16,128]{0,2,1:T(8,128)(2,1)}), bf16[128,16,128]{0,2,1:T(8,128)(2,1)S(1)}, u32[]{:S(2)}, u32[]{:S(2)}) async-start(bf16[128,16,128]{0,2,1:T(8,128)(2,1)} %bitcast.10), calls=%async_computation | async-start | bytes 1048576 | tf_op jit(solution)/shard_map/all_to_all | solution.py:86
  143.5 309.6 %all-gather.11.cloned.1.call-start = ((), (), s32[]{:S(2)}) async-start(), calls=%async_computation.9 | async-start | bytes 1081344 | tf_op jit(solution)/shard_map/all_gather | solution.py:138
  157.1 17.3 %copy-start.4 = (f32[1,64,256]{2,1,0:T(8,128)S(1)}, f32[1,64,256]{2,1,0:T(8,128)}, u32[]{:S(2)}) copy-start(f32[1,64,256]{2,1,0:T(8,128)} %param.24) | copy-start | bytes 196612
  157.2 17.9 %copy-start.5 = (s32[128,8]{0,1:T(8,128)S(1)}, s32[128,8]{0,1:T(8,128)}, u32[]{:S(2)}) copy-start(s32[128,8]{0,1:T(8,128)} %param.26) | copy-start | bytes 12292
  157.2 27.2 %copy-start = (bf16[128,2048]{1,0:T(8,128)(2,1)S(1)}, bf16[128,2048]{1,0:T(8,128)(2,1)}, u32[]{:S(2)}) copy-start(bf16[128,2048]{1,0:T(8,128)(2,1)} %param.15) | copy-start | bytes 1572868
  169.5 14.6 %all-to-all-start.3 = ((bf16[16,128,128]{2,1,0:T(8,128)(2,1)}), bf16[16,128,128]{2,1,0:T(8,128)(2,1)S(1)}, u32[]{:S(2)}, u32[]{:S(2)}) async-start(bf16[16,128,128]{2,1,0:T(8,128)(2,1)} %bitcast.20), calls=%async_computation.3 | async-start | bytes 1048576 | tf_op jit(solution)/shard_map/all_to_all | solution.py:107
  174.4 419.6 %all-gather.9.cloned.1.call-start = ((), (), s32[]{:S(2)}) async-start(), calls=%async_computation.8 | async-start | bytes 1081344 | tf_op jit(solution)/shard_map/all_gather | solution.py:137
  184.4 6.4 %copy-start.9 = (f32[2048]{0:T(1024)S(1)}, f32[2048]{0:T(1024)}, u32[]{:S(2)}) copy-start(f32[2048]{0:T(1024)} %param.22) | copy-start | bytes 24580
  190.8 407.1 %copy-start.1 = (bf16[128,2048]{1,0:T(8,128)(2,1)}, bf16[128,2048]{1,0:T(8,128)(2,1)S(1)}, u32[]{:S(2)}) copy-start(bf16[128,2048]{1,0:T(8,128)(2,1)S(1)} %get-tuple-element.98) | copy-start | bytes 1572868
  190.8 6.4 copy-start.6
  192.3 119.6 %all-to-all-start.4 = ((bf16[16,16,2048]{2,1,0:T(8,128)(2,1)}), bf16[16,16,2048]{2,1,0:T(8,128)(2,1)S(1)}, u32[]{:S(2)}, u32[]{:S(2)}) async-start(bf16[16,16,2048]{2,1,0:T(8,128)(2,1)} %bitcast.24), calls=%async_computation.4 | async-start | bytes 2097152 | tf_op jit(solution)/shard_map/all_to_all | solution.py:140
  197.3 414.6 %copy-start.7 = (s32[1,17]{1,0:T(1,128)S(1)}, s32[1,17]{1,0:T(1,128)}, u32[]{:S(2)}) copy-start(s32[1,17]{1,0:T(1,128)} %param.20) | copy-start | bytes 208
  597.8 29.5 %all-to-all-start.5 = ((bf16[16,16,2048]{2,1,0:T(8,128)(2,1)}), bf16[16,16,2048]{2,1,0:T(8,128)(2,1)S(1)}, u32[]{:S(2)}, u32[]{:S(2)}) async-start(bf16[16,16,2048]{2,1,0:T(8,128)(2,1)} %convolution_convert_fusion), calls=%async_computation.5 | async-start | bytes 2097152 | tf_op jit(solution)/shard_map/all_to_all | solution.py:147
Sparse Core Ops, SparseCore 0:
  85.3 89.7 all-gather.4
  178.1 133.7 all-gather.6
  315.6 137.4 all-gather.10
  456.6 137.4 all-gather.8
where the time goes:
time: 637 us; the launch traced here: 636 us
  waiting for transfers between devices  440 us (69%)
  blocking collectives  77.1 us (12%)
  starting transfers between devices  53.2 us (8%)
  matrix products  23.4 us (4%)
  local copies, waits for them, and re-layouts  20.7 us (3%)
  between operations  14 us (2%)
  other arithmetic  7.47 us (1%)
    all_gather x1, waiting for transfers between devices, body(): lax.all_gather(up_shard.astype(jnp.bfloat16), 'dp', axis=1, tiled=True)  141 us
    all_gather x1, waiting for transfers between devices, body(): lax.all_gather(down_shard.astype(jnp.bfloat16), 'dp', axis=2, tiled=True)  139 us
    all_gather x1, waiting for transfers between devices, body(): lax.all_gather(gate_shard.astype(jnp.bfloat16), 'dp', axis=1, tiled=True)  115 us
    all_gather x1, blocking collectives, body(): columns = lax.all_gather(wo_cast, 'dp', axis=1, tiled=True)  77.1 us
    all_to_all x1, starting transfers between devices, body(): lax.all_to_all(new_keys, 'tensor', split_axis=1, concat_axis=0, tiled=True)  19.2 us
    all_to_all x1, starting transfers between devices, body(): lax.all_to_all(result, 'tensor', split_axis=0, concat_axis=0, tiled=True)  14 us
  transfers between devices with their start and end apart: 10, of which 8 were waited for; matrix products, arithmetic and copies ran while one was open for 7% of the time, Pallas kernels for 0%

commit v1 on v0

--- a/solution.py
+++ b/solution.py
@@ -3,7 +3,7 @@
 import jax
 import jax.numpy as jnp
 from jax import lax
-from jax.sharding import PartitionSpec as P
+from jax.sharding import Mesh, PartitionSpec as P
 
 D = 2048
 HEADS = 16
@@ -63,6 +63,19 @@
         return output.astype(jnp.bfloat16).reshape(block_rows, heads_here * HD)
 
     return lax.map(one_block, (q_blocks, seg_blocks)).reshape(group_rows, heads_here * HD)
+
+
+def gather_dp(pieces):
+    flat = jnp.concatenate([p.reshape(-1) for p in pieces])
+    lanes = 128
+    packed = flat.reshape(-1, lanes)
+    gathered = lax.all_gather(lax.all_gather(packed, "dh"), "dz")
+    gathered = jnp.swapaxes(gathered, 0, 1).reshape(-1, flat.shape[0])
+    out, at = [], 0
+    for p in pieces:
+        out.append(gathered[:, at : at + p.size].reshape((-1,) + p.shape))
+        at += p.size
+    return out
 
 
 def body(
@@ -105,11 +118,21 @@
     )
     attended = attend_group(q_heads, k_heads, v_heads, segment, heads_here)
     token_rows = lax.all_to_all(attended, "tensor", split_axis=0, concat_axis=1, tiled=True)
-    wo_cast = wo_shard.astype(jnp.bfloat16)
-    columns = lax.all_gather(wo_cast, "dp", axis=1, tiled=True)
+    weights_full = gather_dp(
+        [
+            wo_shard.astype(jnp.bfloat16),
+            gate_shard[0].astype(jnp.bfloat16),
+            up_shard[0].astype(jnp.bfloat16),
+            down_shard[0].astype(jnp.bfloat16),
+        ]
+    )
+    wo_rows = weights_full[0].transpose(1, 0, 2).reshape(wo_shard.shape[0], -1)
+    gate_full = weights_full[1].reshape(1, -1, gate_shard.shape[2])
+    up_full = weights_full[2].reshape(1, -1, up_shard.shape[2])
+    down_full = weights_full[3].transpose(1, 0, 2).reshape(1, down_shard.shape[1], -1)
     projected = jnp.dot(
         token_rows,
-        lax.all_gather(columns, "tensor", axis=0, tiled=True),
+        lax.all_gather(wo_rows, "tensor", axis=0, tiled=True),
         preferred_element_type=jnp.float32,
     )
     hidden_mid = (residual.astype(jnp.float32) + projected).astype(jnp.bfloat16)
@@ -132,11 +155,6 @@
         "tem,td->emd", picked.astype(jnp.bfloat16), normed, preferred_element_type=jnp.float32
     ).astype(jnp.bfloat16)
     outgoing = jnp.repeat(outgoing, SPLIT, axis=0)
-    gate_full, up_full, down_full = (
-        lax.all_gather(gate_shard.astype(jnp.bfloat16), "dp", axis=1, tiled=True),
-        lax.all_gather(up_shard.astype(jnp.bfloat16), "dp", axis=1, tiled=True),
-        lax.all_gather(down_shard.astype(jnp.bfloat16), "dp", axis=2, tiled=True),
-    )
     arrived = lax.all_to_all(outgoing, "tensor", split_axis=0, concat_axis=0, tiled=True)
     gate_val = jnp.einsum("smd,dp->smp", arrived, gate_full[0], preferred_element_type=jnp.float32)
     up_val = jnp.einsum("smd,dp->smp", arrived, up_full[0], preferred_element_type=jnp.float32)
@@ -154,29 +172,35 @@
 
 
 def solution(mesh):
+    dp_count = mesh.shape["dp"]
+    dz_count = 16 if dp_count % 16 == 0 else dp_count
+    split_mesh = Mesh(
+        mesh.devices.reshape(dp_count // dz_count, dz_count, mesh.shape["tensor"]),
+        ("dh", "dz", "tensor"),
+    )
     return jax.shard_map(
         body,
-        mesh=mesh,
+        mesh=split_mesh,
         in_specs=(
-            P(("dp", "tensor"), None),
-            P(("dp", "tensor"), None),
-            P(("dp", "tensor"), None),
-            P(("dp", "tensor"), None),
-            P("dp", None),
-            P("dp", None),
-            P("tensor", "dp"),
+            P(("dh", "dz", "tensor"), None),
+            P(("dh", "dz", "tensor"), None),
+            P(("dh", "dz", "tensor"), None),
+            P(("dh", "dz", "tensor"), None),
+            P(("dh", "dz"), None),
+            P(("dh", "dz"), None),
+            P("tensor", ("dh", "dz")),
             P(),
-            P("tensor", "dp", None),
-            P("tensor", "dp", None),
-            P("tensor", None, "dp"),
-            P(("dp", "tensor"), None),
-            P(("dp", "tensor"), None),
+            P("tensor", ("dh", "dz"), None),
+            P("tensor", ("dh", "dz"), None),
+            P("tensor", None, ("dh", "dz")),
+            P(("dh", "dz", "tensor"), None),
+            P(("dh", "dz", "tensor"), None),
         ),
         out_specs=(
-            P(("dp", "tensor"), None),
-            P(("dp", "tensor"), None),
-            P("dp", None, "tensor"),
-            P("dp", None, "tensor"),
+            P(("dh", "dz", "tensor"), None),
+            P(("dh", "dz", "tensor"), None),
+            P(("dh", "dz"), None, "tensor"),
+            P(("dh", "dz"), None, "tensor"),
         ),
         check_vma=False,
     )

time: 637 us -> 257 us (0.40)
  waiting for transfers between devices: 440 us -> 128 us
  blocking collectives: 77.1 us -> 6.67 us
  local copies, waits for them, and re-layouts: 20.7 us -> 39.2 us
  starting transfers between devices: 53.2 us -> 37.5 us
    all_gather x4 -> x2, waiting for transfers between devices: 395 us -> 76 us  [the longest x1 73.5 us: gather_dp(): gathered = lax.all_gather(lax.all_gather(packed, 'dh'), 'dz')]
    all_gather x1, blocking collectives: 77.1 us -> 6.67 us  [gather_dp(): gathered = lax.all_gather(lax.all_gather(packed, 'dh'), 'dz')]
    all_to_all x1, starting transfers between devices: 14 us -> 4.5 us  [body(): lax.all_to_all(result, 'tensor', split_axis=0, concat_axis=0, tiled=True)]
  transfers between devices with their start and end apart: 10 -> 8, of which waited for: 8 -> 8; matrix products, arithmetic and copies ran while one was open for 7% -> 16% of each run, Pallas kernels for 0% -> 0%
where the time goes in v1:
time: 257 us; the launch traced here: 256 us
  waiting for transfers between devices  128 us (50%)
  local copies, waits for them, and re-layouts  39.2 us (15%)
  starting transfers between devices  37.5 us (15%)
  matrix products  23.4 us (9%)
  between operations  14.4 us (6%)
  other arithmetic  7.29 us (3%)
  blocking collectives  6.67 us (3%)
    all_gather x1, waiting for transfers between devices, gather_dp(): gathered = lax.all_gather(lax.all_gather(packed, 'dh'), 'dz')  73.5 us
    all_to_all x1, starting transfers between devices, body(): lax.all_to_all(new_keys, 'tensor', split_axis=1, concat_axis=0, tiled=True)  15.2 us
    all_to_all x1, waiting for transfers between devices, body(): lax.all_to_all(new_values, 'tensor', split_axis=1, concat_axis=0, tiled=T...  13.2 us
    all_to_all x1, waiting for transfers between devices, body(): lax.all_to_all(queries, 'tensor', split_axis=1, concat_axis=0, tiled=True)  12.4 us
    all_to_all x1, waiting for transfers between devices, body(): lax.all_to_all(attended, 'tensor', split_axis=0, concat_axis=1, tiled=True)  10.6 us
    all_to_all x1, waiting for transfers between devices, body(): lax.all_to_all(new_keys, 'tensor', split_axis=1, concat_axis=0, tiled=True)  8.79 us
    unnamed x32, local copies, waits for them, and re-layouts  7.32 us
    scatter x1, local copies, waits for them, and re-layouts, body(): key_pages = jnp.zeros((pool_size * PAGE, head_width), jnp.bfloat16).at[sl...  6.88 us
  transfers between devices with their start and end apart: 8, of which 8 were waited for; matrix products, arithmetic and copies ran while one was open for 16% of the time, Pallas kernels for 0%

profile of v1, /device:TPU:1, one launch (start us, length us, event | category | flops | bytes accessed | tf_op | source)
XLA Modules:
  0.0 256.0 jit_solution(10472110182598479240)
XLA Ops:
  11.0 6.7 %all_gather.12 = bf16[2,448,128]{2,1,0:T(8,128)(2,1)} all-gather(bf16[1,448,128]{2,1,0:T(8,128)(2,1)S(1)} %maximum_bitcast_fusion), channel_id=1, replica_groups=mesh['dh'=2,'dz'=16,'tensor'=16] {'dh'}, dimensions={0}, use_global_device_ids=true | all-gather | bytes 344064 | tf_op jit(solution)/shard_map/all_gather | solution.py:72
  17.8 73.5 %all-gather.6.cloned.1.call-done = bf16[32,448,128]{2,1,0:T(8,128)(2,1)} async-done(((bf16[2,448,128]{2,1,0:T(8,128)(2,1)}), bf16[32,448,128]{2,1,0:T(8,128)(2,1)}) %all-gather.6.cloned.1.call-update) | async-done | bytes 3670032 | tf_op jit(solution)/shard_map/all_gather | solution.py:72
  91.3 2.3 copy.103
  93.6 2.4 copy.117
  101.2 15.2 %all-to-all-start.1 = ((bf16[128,16,128]{0,2,1:T(8,128)(2,1)}), bf16[128,16,128]{0,2,1:T(8,128)(2,1)S(1)}, u32[]{:S(2)}, u32[]{:S(2)}) async-start(bf16[128,16,128]{0,2,1:T(8,128)(2,1)} %bitcast.14), calls=%async_computation.1 | async-start | bytes 1048576 | tf_op jit(solution)/shard_map/all_to_all | solution.py:100
  117.4 8.8 %all-to-all-done.1 = bf16[128,16,128]{0,2,1:T(8,128)(2,1)S(1)} async-done(((bf16[128,16,128]{0,2,1:T(8,128)(2,1)}), bf16[128,16,128]{0,2,1:T(8,128)(2,1)S(1)}, u32[]{:S(2)}, u32[]{:S(2)}) %all-to-all-start.1) | async-done | bytes 524320 | tf_op jit(solution)/shard_map/all_to_all | solution.py:100
  126.2 4.5 %all-to-all-start.2 = ((bf16[128,16,128]{0,2,1:T(8,128)(2,1)}), bf16[128,16,128]{0,2,1:T(8,128)(2,1)S(1)}, u32[]{:S(2)}, u32[]{:S(2)}) async-start(bf16[128,16,128]{0,2,1:T(8,128)(2,1)} %bitcast.17), calls=%async_computation.2 | async-start | bytes 1048576 | tf_op jit(solution)/shard_map/all_to_all | solution.py:101
  131.7 13.2 %all-to-all-done.2 = bf16[128,16,128]{0,2,1:T(8,128)(2,1)S(1)} async-done(((bf16[128,16,128]{0,2,1:T(8,128)(2,1)}), bf16[128,16,128]{0,2,1:T(8,128)(2,1)S(1)}, u32[]{:S(2)}, u32[]{:S(2)}) %all-to-all-start.2) | async-done | bytes 524320 | tf_op jit(solution)/shard_map/all_to_all | solution.py:101
  144.9 4.4 %all-to-all-start = ((bf16[128,16,128]{0,2,1:T(8,128)(2,1)}), bf16[128,16,128]{0,2,1:T(8,128)(2,1)S(1)}, u32[]{:S(2)}, u32[]{:S(2)}) async-start(bf16[128,16,128]{0,2,1:T(8,128)(2,1)} %bitcast.10), calls=%async_computation | async-start | bytes 1048576 | tf_op jit(solution)/shard_map/all_to_all | solution.py:99
  150.5 12.4 %all-to-all-done = bf16[128,16,128]{0,2,1:T(8,128)(2,1)S(1)} async-done(((bf16[128,16,128]{0,2,1:T(8,128)(2,1)}), bf16[128,16,128]{0,2,1:T(8,128)(2,1)S(1)}, u32[]{:S(2)}, u32[]{:S(2)}) %all-to-all-start) | async-done | bytes 524320 | tf_op jit(solution)/shard_map/all_to_all | solution.py:99
  163.2 12.2 %while.10 = (s32[]{:T(128)}, bf16[4,512,128]{2,1,0:T(8,128)(2,1)}, s32[4,512]{1,0:T(4,128)S(1)}, s32[2048]{0:T(1024)S(1)}, bf16[4,512,1,128]{3,1,2,0:T(8,128)(2,...) while((s32[]{:T(128)}, bf16[4,512,128]{2,1,0:T(8,128)(2,1)}, ...), condition=%wide.region_5.6_spmd, body=%wide.region_2.0_spmd.sunk | while | flops 545389568 | bytes 13918813 | solution.py:65
  175.5 4.5 %all-to-all-start.3 = ((bf16[16,128,128]{2,1,0:T(8,128)(2,1)}), bf16[16,128,128]{2,1,0:T(8,128)(2,1)S(1)}, u32[]{:S(2)}, u32[]{:S(2)}) async-start(bf16[16,128,128]{2,1,0:T(8,128)(2,1)} %bitcast.20), calls=%async_computation.3 | async-start | bytes 1048576 | tf_op jit(solution)/shard_map/all_to_all | solution.py:120
  180.3 10.6 %all-to-all-done.3 = bf16[16,128,128]{2,1,0:T(8,128)(2,1)S(1)} async-done(((bf16[16,128,128]{2,1,0:T(8,128)(2,1)}), bf16[16,128,128]{2,1,0:T(8,128)(2,1)S(1)}, u32[]{:S(2)}, u32[]{:S(2)}) %all-to-all-start.3) | async-done | bytes 524320 | tf_op jit(solution)/shard_map/all_to_all | solution.py:120
  191.2 2.5 all-gather.4.cloned.1.call-done
  193.7 6.4 %fusion.28 = (f32[128]{0:T(128)S(1)}, bf16[128,2048]{1,0:T(8,128)(2,1)S(1)}) fusion(bf16[128,2048]{0,1:T(8,128)(2,1)S(1)} %bitcast.126, bf16[2048,2048]{0,1:T(8,128)(2,1)} %all-gather.4.cloned.1.call-done, bf16[128,2048]{1,0:T(8,128)(2,1)S(1)} %copy-done.2), kind=kOutput, calls=%fused_computation.31 | convolution fusion | flops 1075314560 | bytes 9961984 | tf_op jit(solution)/shard_map/dot_general | solution.py:133
  201.6 4.3 %all-to-all-start.4 = ((bf16[16,16,2048]{2,1,0:T(8,128)(2,1)}), bf16[16,16,2048]{2,1,0:T(8,128)(2,1)}, u32[]{:S(2)}, u32[]{:S(2)}) async-start(bf16[16,16,2048]{2,1,0:T(8,128)(2,1)} %bitcast.29), calls=%async_computation.4 | async-start | bytes 2097152 | tf_op jit(solution)/shard_map/all_to_all | solution.py:158
  205.9 3.4 %fusion.66 = (bf16[32,16384]{1,0:T(8,128)(2,1)S(1)}, bf16[32,16384]{1,0:T(8,128)(2,1)}, bf16[32,16384]{1,0:T(8,128)(2,1)}) fusion(bf16[32,57344]{1,0:T(8,128)(2,1)} %bitcast.120), kind=kLoop, calls=%fused_computation.97 | loop fusion | bytes 6291456 | tf_op jit(solution)/shard_map/slice | solution.py:76
  210.6 3.0 %reshape.260 = bf16[32,256,64]{2,1,0:T(8,128)(2,1)S(1)} reshape(bf16[32,16384]{1,0:T(8,128)(2,1)} %get-tuple-element.96) | data formatting | bytes 2097152 | tf_op jit(solution)/shard_map/reshape | solution.py:76
  217.0 4.6 %all-to-all-done.4 = bf16[16,16,2048]{2,1,0:T(8,128)(2,1)} async-done(((bf16[16,16,2048]{2,1,0:T(8,128)(2,1)}), bf16[16,16,2048]{2,1,0:T(8,128)(2,1)}, u32[]{:S(2)}, u32[]{:S(2)}) %all-to-all-start.4) | async-done | bytes 1048608 | tf_op jit(solution)/shard_map/all_to_all | solution.py:158
  221.6 2.0 fusion.67
  223.6 3.5 %convolution_convert_fusion = bf16[16,16,2048]{2,1,0:T(8,128)(2,1)} fusion(bf16[256,2048,1]{0,1,2:T(8,128)(2,1)S(1)} %bitcast.131, bf16[16,16,2048]{2,1,0:T(8,128)(2,1)} %all-to-all-done.4, bf16[2048,256,1]{1,0,2:T(8,128)(2,1)S(1)} %reshape.284, f32[16,16,256]{2,1,0:T(8,128)S(1)} %fusion.67), kind=kOutput, calls=%fused_computation.20 | convolution fusion | flops 537788416 | bytes 4456448 | tf_op jit(solution)/shard_map/smp,pd->smd/dot_general | solution.py:162
  227.1 4.5 %all-to-all-start.5 = ((bf16[16,16,2048]{2,1,0:T(8,128)(2,1)}), bf16[16,16,2048]{2,1,0:T(8,128)(2,1)S(1)}, u32[]{:S(2)}, u32[]{:S(2)}) async-start(bf16[16,16,2048]{2,1,0:T(8,128)(2,1)} %convolution_convert_fusion), calls=%async_computation.5 | async-start | bytes 2097152 | tf_op jit(solution)/shard_map/all_to_all | solution.py:165
  231.8 6.9 %scatter_custom_fusion = bf16[2176,128]{1,0:T(8,128)(2,1)} fusion(s32[2048]{0:T(1024)S(1)} %bitcast.142, bf16[2048,128]{1,0:T(8,128)(2,1)} %bitcast.135, bf16[]{:T(256)} %constant.81.clone.1), kind=kCustom, calls=%fused_computation.39 | custom fusion | bytes 557568 | tf_op jit(solution)/shard_map/scatter | solution.py:110
  238.7 6.5 %scatter_custom_fusion.1 = bf16[2176,128]{1,0:T(8,128)(2,1)} fusion(s32[2048]{0:T(1024)S(1)} %bitcast.143, bf16[2048,128]{1,0:T(8,128)(2,1)S(1)} %bitcast.118, bf16[]{:T(256)} %constant.81.clone.1), kind=kCustom, calls=%fused_computation.37 | custom fusion | bytes 557058 | tf_op jit(solution)/shard_map/scatter | solution.py:116
  (95 shorter events, 35.6 us)
Async XLA Ops:
  7.2 84.1 %all-gather.6.cloned.1.call-start = ((), (), s32[]{:S(2)}) async-start(), calls=%async_computation.7 | async-start | bytes 3899392 | tf_op jit(solution)/shard_map/all_gather | solution.py:72
  17.7 175.9 %all-gather.4.cloned.1.call-start = ((), (), s32[]{:S(2)}) async-start(), calls=%async_computation.6 | async-start | bytes 8912896 | tf_op jit(solution)/shard_map/all_gather | solution.py:135
  96.0 1.9 copy-start
  96.0 4.2 %copy-start.4 = (bf16[128,2048]{1,0:T(8,128)(2,1)S(1)}, bf16[128,2048]{1,0:T(8,128)(2,1)}, u32[]{:S(2)}) copy-start(bf16[128,2048]{1,0:T(8,128)(2,1)} %param.17) | copy-start | bytes 1572868
  96.0 20.4 %copy-start.5 = (bf16[128,2048]{1,0:T(8,128)(2,1)S(1)}, bf16[128,2048]{1,0:T(8,128)(2,1)}, u32[]{:S(2)}) copy-start(bf16[128,2048]{1,0:T(8,128)(2,1)} %param.18) | copy-start | bytes 1572868
  97.9 32.8 %copy-start.6 = (bf16[128,2048]{1,0:T(8,128)(2,1)S(1)}, bf16[128,2048]{1,0:T(8,128)(2,1)}, u32[]{:S(2)}) copy-start(bf16[128,2048]{1,0:T(8,128)(2,1)} %param.16) | copy-start | bytes 1572868
  99.0 50.3 %copy-start.11 = (s32[1,2]{1,0:T(1,128)S(1)}, s32[1,2]{1,0:T(1,128)}, u32[]{:S(2)}) copy-start(s32[1,2]{1,0:T(1,128)} %param.19) | copy-start | bytes 28
  99.0 50.6 %copy-start.8 = (s32[128,8]{0,1:T(8,128)S(1)}, s32[128,8]{0,1:T(8,128)}, u32[]{:S(2)}) copy-start(s32[128,8]{0,1:T(8,128)} %param.26) | copy-start | bytes 12292
  101.2 25.0 %all-to-all-start.1 = ((bf16[128,16,128]{0,2,1:T(8,128)(2,1)}), bf16[128,16,128]{0,2,1:T(8,128)(2,1)S(1)}, u32[]{:S(2)}, u32[]{:S(2)}) async-start(bf16[128,16,128]{0,2,1:T(8,128)(2,1)} %bitcast.14), calls=%async_computation.1 | async-start | bytes 1048576 | tf_op jit(solution)/shard_map/all_to_all | solution.py:100
  126.2 18.7 %all-to-all-start.2 = ((bf16[128,16,128]{0,2,1:T(8,128)(2,1)}), bf16[128,16,128]{0,2,1:T(8,128)(2,1)S(1)}, u32[]{:S(2)}, u32[]{:S(2)}) async-start(bf16[128,16,128]{0,2,1:T(8,128)(2,1)} %bitcast.17), calls=%async_computation.2 | async-start | bytes 1048576 | tf_op jit(solution)/shard_map/all_to_all | solution.py:101
  144.9 18.0 %all-to-all-start = ((bf16[128,16,128]{0,2,1:T(8,128)(2,1)}), bf16[128,16,128]{0,2,1:T(8,128)(2,1)S(1)}, u32[]{:S(2)}, u32[]{:S(2)}) async-start(bf16[128,16,128]{0,2,1:T(8,128)(2,1)} %bitcast.10), calls=%async_computation | async-start | bytes 1048576 | tf_op jit(solution)/shard_map/all_to_all | solution.py:99
  163.2 17.0 %copy-start.9 = (f32[128,8]{0,1:T(8,128)S(1)}, f32[128,8]{0,1:T(8,128)}, u32[]{:S(2)}) copy-start(f32[128,8]{0,1:T(8,128)} %param.27) | copy-start | bytes 12292
  163.2 30.5 %copy-start.2 = (bf16[128,2048]{1,0:T(8,128)(2,1)S(1)}, bf16[128,2048]{1,0:T(8,128)(2,1)}, u32[]{:S(2)}) copy-start(bf16[128,2048]{1,0:T(8,128)(2,1)} %param.15) | copy-start | bytes 1572868
  175.5 24.6 %copy-start.7 = (bf16[2048,1,128]{2,0,1:T(8,128)(2,1)}, bf16[2048,1,128]{2,0,1:T(8,128)(2,1)S(1)}, u32[]{:S(2)}) copy-start(bf16[2048,1,128]{2,0,1:T(8,128)(2,1)S(1)} %get-tuple-element.187) | copy-start | bytes 1572868
  175.5 15.5 %all-to-all-start.3 = ((bf16[16,128,128]{2,1,0:T(8,128)(2,1)}), bf16[16,128,128]{2,1,0:T(8,128)(2,1)S(1)}, u32[]{:S(2)}, u32[]{:S(2)}) async-start(bf16[16,128,128]{2,1,0:T(8,128)(2,1)} %bitcast.20), calls=%async_computation.3 | async-start | bytes 1048576 | tf_op jit(solution)/shard_map/all_to_all | solution.py:120
  193.7 6.4 %copy-start.12 = (f32[2048]{0:T(1024)S(1)}, f32[2048]{0:T(1024)}, u32[]{:S(2)}) copy-start(f32[2048]{0:T(1024)} %param.22) | copy-start | bytes 24580
  200.1 9.3 %copy-start.3 = (bf16[128,2048]{1,0:T(8,128)(2,1)}, bf16[128,2048]{1,0:T(8,128)(2,1)S(1)}, u32[]{:S(2)}) copy-start(bf16[128,2048]{1,0:T(8,128)(2,1)S(1)} %get-tuple-element.101) | copy-start | bytes 1572868
  201.6 20.0 %all-to-all-start.4 = ((bf16[16,16,2048]{2,1,0:T(8,128)(2,1)}), bf16[16,16,2048]{2,1,0:T(8,128)(2,1)}, u32[]{:S(2)}, u32[]{:S(2)}) async-start(bf16[16,16,2048]{2,1,0:T(8,128)(2,1)} %bitcast.29), calls=%async_computation.4 | async-start | bytes 2097152 | tf_op jit(solution)/shard_map/all_to_all | solution.py:158
  215.3 8.3 %copy-start.1 = (bf16[256,32,64]{0,2,1:T(8,128)(2,1)S(1)}, bf16[256,32,64]{0,2,1:T(8,128)(2,1)}, u32[]{:S(2)}) copy-start(bf16[256,32,64]{0,2,1:T(8,128)(2,1)} %copy.107) | copy-start | bytes 3145732
  217.0 14.7 %copy-start.10 = (s32[1,17]{1,0:T(1,128)S(1)}, s32[1,17]{1,0:T(1,128)}, u32[]{:S(2)}) copy-start(s32[1,17]{1,0:T(1,128)} %param.20) | copy-start | bytes 208
  227.1 20.1 %all-to-all-start.5 = ((bf16[16,16,2048]{2,1,0:T(8,128)(2,1)}), bf16[16,16,2048]{2,1,0:T(8,128)(2,1)S(1)}, u32[]{:S(2)}, u32[]{:S(2)}) async-start(bf16[16,16,2048]{2,1,0:T(8,128)(2,1)} %convolution_convert_fusion), calls=%async_computation.5 | async-start | bytes 2097152 | tf_op jit(solution)/shard_map/all_to_all | solution.py:165
Sparse Core Ops, SparseCore 0:
  17.9 73.3 all-gather.5
  100.3 93.3 all-gather.3

commit v2 on v1

--- a/solution.py
+++ b/solution.py
@@ -76,6 +76,24 @@
         out.append(gathered[:, at : at + p.size].reshape((-1,) + p.shape))
         at += p.size
     return out
+
+
+def ring_gather(block, axis):
+    n = lax.axis_size(axis)
+    me = lax.axis_index(axis)
+    fwd = [(i, (i + 1) % n) for i in range(n)]
+    bwd = [(i, (i - 1) % n) for i in range(n)]
+    relative = [None] * n
+    relative[0] = block
+    a = b = block
+    for step in range(n // 2):
+        a = lax.ppermute(a, axis, fwd)
+        relative[n - 1 - step] = a
+        if step + 1 < n - 1 - step:
+            b = lax.ppermute(b, axis, bwd)
+            relative[step + 1] = b
+    stacked = jnp.stack(relative + relative)
+    return lax.dynamic_slice_in_dim(stacked, n - me, n, axis=0)
 
 
 def body(
@@ -116,20 +134,30 @@
         .set(v_heads)
         .reshape(pool_size, PAGE, head_width)
     )
+    k_heads, v_heads, key_pages, value_pages = lax.optimization_barrier(
+        (k_heads, v_heads, key_pages, value_pages)
+    )
     attended = attend_group(q_heads, k_heads, v_heads, segment, heads_here)
     token_rows = lax.all_to_all(attended, "tensor", split_axis=0, concat_axis=1, tiled=True)
-    weights_full = gather_dp(
-        [
-            wo_shard.astype(jnp.bfloat16),
-            gate_shard[0].astype(jnp.bfloat16),
-            up_shard[0].astype(jnp.bfloat16),
-            down_shard[0].astype(jnp.bfloat16),
-        ]
-    )
-    wo_rows = weights_full[0].transpose(1, 0, 2).reshape(wo_shard.shape[0], -1)
-    gate_full = weights_full[1].reshape(1, -1, gate_shard.shape[2])
-    up_full = weights_full[2].reshape(1, -1, up_shard.shape[2])
-    down_full = weights_full[3].transpose(1, 0, 2).reshape(1, down_shard.shape[1], -1)
+    wo_full = gather_dp([wo_shard.astype(jnp.bfloat16)])[0]
+    wo_rows = wo_full.transpose(1, 0, 2).reshape(wo_shard.shape[0], -1)
+    expert_pieces = [
+        gate_shard[0].astype(jnp.bfloat16),
+        up_shard[0].astype(jnp.bfloat16),
+        down_shard[0].astype(jnp.bfloat16),
+    ]
+    expert_flat = jnp.concatenate([p.reshape(-1) for p in expert_pieces]).reshape(-1, 128)
+    expert_pairs = lax.all_gather(expert_flat, "dh")
+    expert_all = jnp.swapaxes(ring_gather(expert_pairs, "dz"), 0, 1)
+    expert_all = expert_all.reshape(-1, expert_flat.size)
+    at = 0
+    weights_full = []
+    for p in expert_pieces:
+        weights_full.append(expert_all[:, at : at + p.size].reshape((-1,) + p.shape))
+        at += p.size
+    gate_full = weights_full[0].reshape(1, -1, gate_shard.shape[2])
+    up_full = weights_full[1].reshape(1, -1, up_shard.shape[2])
+    down_full = weights_full[2].transpose(1, 0, 2).reshape(1, down_shard.shape[1], -1)
     projected = jnp.dot(
         token_rows,
         lax.all_gather(wo_rows, "tensor", axis=0, tiled=True),

time: 257 us -> 308 us (1.20)
  waiting for transfers between devices: 128 us -> 58.9 us
  starting transfers between devices: 37.5 us -> 92.2 us
  blocking collectives: 6.67 us -> 43.1 us
  local copies, waits for them, and re-layouts: 39.2 us -> 62.4 us
  matrix products: 23.4 us -> 27.8 us
    all_gather x1 -> x0, waiting for transfers between devices: 73.5 us -> none  [gather_dp(): gathered = lax.all_gather(lax.all_gather(packed, 'dh'), 'dz')]
    ppermute x0 -> x15, starting transfers between devices: none -> 47.3 us  [the longest x7 30.3 us: ring_gather(): b = lax.ppermute(b, axis, bwd)]
    all_gather x1 -> x2, blocking collectives: 6.67 us -> 37.5 us  [gather_dp(): gathered = lax.all_gather(lax.all_gather(packed, 'dh'), 'dz')]
    unnamed x32 -> x57, local copies, waits for them, and re-layouts: 7.32 us -> 29.1 us
    ppermute x0 -> x15, waiting for transfers between devices: none -> 13.8 us  [the longest x8 9.83 us: ring_gather(): a = lax.ppermute(a, axis, fwd)]
    all_to_all x1, waiting for transfers between devices: 1.96 us -> 15.5 us  [body(): lax.all_to_all(result, 'tensor', split_axis=0, concat_axis=0, tiled=True)]
    all_to_all x1, waiting for transfers between devices: 12.4 us -> 0.01 us  [body(): lax.all_to_all(queries, 'tensor', split_axis=1, concat_axis=0, tiled=True)]
    all_to_all x1, waiting for transfers between devices: 10.6 us -> 0.01 us  [body(): lax.all_to_all(attended, 'tensor', split_axis=0, concat_axis=1, tiled=True)]
  transfers between devices with their start and end apart: 8 -> 22, of which waited for: 8 -> 9; matrix products, arithmetic and copies ran while one was open for 16% -> 26% of each run, Pallas kernels for 0% -> 0%
where the time goes in v2:
time: 308 us; the launch traced here: 306 us
  starting transfers between devices  92.2 us (30%)
  local copies, waits for them, and re-layouts  62.4 us (20%)
  waiting for transfers between devices  58.9 us (19%)
  blocking collectives  43.1 us (14%)
  matrix products  27.8 us (9%)
  between operations  14.5 us (5%)
  other arithmetic  7.38 us (2%)
    all_gather x2, blocking collectives, gather_dp(): gathered = lax.all_gather(lax.all_gather(packed, 'dh'), 'dz')  37.5 us
    ppermute x7, starting transfers between devices, ring_gather(): b = lax.ppermute(b, axis, bwd)  30.3 us
    unnamed x57, local copies, waits for them, and re-layouts  29.1 us
    ppermute x8, starting transfers between devices, ring_gather(): a = lax.ppermute(a, axis, fwd)  17 us
    all_to_all x1, waiting for transfers between devices, body(): lax.all_to_all(result, 'tensor', split_axis=0, concat_axis=0, tiled=True)  15.5 us
    all_to_all x1, starting transfers between devices, body(): lax.all_to_all(new_keys, 'tensor', split_axis=1, concat_axis=0, tiled=True)  15.4 us
    all_to_all x1, waiting for transfers between devices, body(): lax.all_to_all(new_keys, 'tensor', split_axis=1, concat_axis=0, tiled=True)  12.7 us
    all_to_all x1, waiting for transfers between devices, body(): lax.all_to_all(new_values, 'tensor', split_axis=1, concat_axis=0, tiled=T...  12.2 us
  transfers between devices with their start and end apart: 22, of which 9 were waited for; matrix products, arithmetic and copies ran while one was open for 26% of the time, Pallas kernels for 0%

profile of v2, /device:TPU:1, one launch (start us, length us, event | category | flops | bytes accessed | tf_op | source)
XLA Modules:
  0.0 306.4 jit_solution(14661807108955243039)
XLA Ops:
  8.4 5.5 %all_gather.15 = bf16[2,64,128]{2,1,0:T(8,128)(2,1)S(1)} all-gather(bf16[1,64,128]{2,1,0:T(8,128)(2,1)S(1)} %all_gather_reshape_reshape.3), channel_id=1, replica_groups=mesh['dh'=2,'dz'=16,'tensor'=16] {'dh'}, dimensions={0}, use_global_device_ids=true | all-gather | bytes 49152 | tf_op jit(solution)/shard_map/all_gather | solution.py:72
  13.9 32.0 %all-gather = bf16[32,64,128]{2,1,0:T(8,128)(2,1)S(1)} all-gather(bf16[2,64,128]{2,1,0:T(8,128)(2,1)S(1)} %all_gather.15), channel_id=2, replica_groups=mesh['dh'=2,'dz'=16,'tensor'=16] {'dz'}, dimensions={0}, use_global_device_ids=true | all-gather | bytes 557056 | tf_op jit(solution)/shard_map/all_gather | solution.py:72
  50.3 5.6 %all_gather.19 = bf16[2,384,128]{2,1,0:T(8,128)(2,1)S(1)} all-gather(bf16[1,384,128]{2,1,0:T(8,128)(2,1)S(1)} %maximum_bitcast_fusion), channel_id=1, replica_groups=mesh['dh'=2,'dz'=16,'tensor'=16] {'dh'}, dimensions={0}, use_global_device_ids=true | all-gather | bytes 294912 | tf_op jit(solution)/shard_map/all_gather | solution.py:150
  62.2 15.4 %all-to-all-start.1 = ((bf16[128,16,128]{2,0,1:T(8,128)(2,1)}), bf16[128,16,128]{2,0,1:T(8,128)(2,1)S(1)}, u32[]{:S(2)}, u32[]{:S(2)}) async-start(bf16[128,16,128]{2,0,1:T(8,128)(2,1)} %copy_bitcast_fusion.2), calls=%async_computation.1 | async-start | bytes 1048576 | tf_op jit(solution)/shard_map/all_to_all | solution.py:118
  79.3 12.7 %all-to-all-done.1 = bf16[128,16,128]{2,0,1:T(8,128)(2,1)S(1)} async-done(((bf16[128,16,128]{2,0,1:T(8,128)(2,1)}), bf16[128,16,128]{2,0,1:T(8,128)(2,1)S(1)}, u32[]{:S(2)}, u32[]{:S(2)}) %all-to-all-start.1) | async-done | bytes 524320 | tf_op jit(solution)/shard_map/all_to_all | solution.py:118
  92.9 4.3 %all-to-all-start.2 = ((bf16[128,16,128]{2,0,1:T(8,128)(2,1)}), bf16[128,16,128]{2,0,1:T(8,128)(2,1)S(1)}, u32[]{:S(2)}, u32[]{:S(2)}) async-start(bf16[128,16,128]{2,0,1:T(8,128)(2,1)} %copy_bitcast_fusion.1), calls=%async_computation.2 | async-start | bytes 1048576 | tf_op jit(solution)/shard_map/all_to_all | solution.py:119
  98.5 12.2 %all-to-all-done.2 = bf16[128,16,128]{2,0,1:T(8,128)(2,1)S(1)} async-done(((bf16[128,16,128]{2,0,1:T(8,128)(2,1)}), bf16[128,16,128]{2,0,1:T(8,128)(2,1)S(1)}, u32[]{:S(2)}, u32[]{:S(2)}) %all-to-all-start.2) | async-done | bytes 524320 | tf_op jit(solution)/shard_map/all_to_all | solution.py:119
  123.7 4.7 %collective-permute-start.2 = (bf16[2,384,128]{2,1,0:T(8,128)(2,1)S(1)}, bf16[2,384,128]{2,1,0:T(8,128)(2,1)S(1)}, u32[]{:S(2)}, u32[]{:S(2)}) collective-permute-start(bf16[2,384,128]{2,1,0:T(8,128)(2,1)S(1)} %collective-permute-done.1), channel_id=1, source_target_pairs={{0,240},{16,0},{32,16},{48,32},{64,48},{80,64},{96,80},{112,96},{1... | collective-permute-start | bytes 589832 | tf_op jit(solution)/shard_map/ppermute | solution.py:93
  130.3 6.9 %scatter_custom_fusion = bf16[2176,128]{1,0:T(8,128)(2,1)} fusion(s32[2048]{0:T(1024)S(1)} %bitcast.203, bf16[2048,128]{1,0:T(8,128)(2,1)} %bitcast.195, bf16[]{:T(256)} %constant.87.clone.1), kind=kCustom, calls=%fused_computation.43 | custom fusion | bytes 557568 | tf_op jit(solution)/shard_map/scatter | solution.py:128
  137.2 6.5 %scatter_custom_fusion.1 = bf16[2176,128]{1,0:T(8,128)(2,1)} fusion(s32[2048]{0:T(1024)S(1)} %bitcast.204, bf16[2048,128]{1,0:T(8,128)(2,1)S(1)} %bitcast.180, bf16[]{:T(256)} %constant.87.clone.1), kind=kCustom, calls=%fused_computation.41 | custom fusion | bytes 557058 | tf_op jit(solution)/shard_map/scatter | solution.py:134
  144.0 16.3 %while.10 = (s32[]{:T(128)}, bf16[4,512,128]{2,1,0:T(8,128)(2,1)}, s32[4,512]{1,0:T(4,128)S(1)}, s32[2048]{0:T(1024)S(1)}, bf16[4,512,1,128]{3,1,2,0:T(8,128)(2,...) while((s32[]{:T(128)}, bf16[4,512,128]{2,1,0:T(8,128)(2,1)}, ...), condition=%wide.region_11.12_spmd, body=%wide.region_8.11_spmd.sunk | while | flops 545389568 | bytes 13918813 | solution.py:65
  160.3 6.6 %all-to-all-start.3 = ((bf16[16,128,128]{2,1,0:T(8,128)(2,1)}), bf16[16,128,128]{2,1,0:T(8,128)(2,1)S(1)}, u32[]{:S(2)}, u32[]{:S(2)}) async-start(bf16[16,128,128]{2,1,0:T(8,128)(2,1)} %bitcast.31), calls=%async_computation.3 | async-start | bytes 1048576 | tf_op jit(solution)/shard_map/all_to_all | solution.py:141
  167.6 4.8 %collective-permute-start.3 = (bf16[2,384,128]{2,1,0:T(8,128)(2,1)S(1)}, bf16[2,384,128]{2,1,0:T(8,128)(2,1)S(1)}, u32[]{:S(2)}, u32[]{:S(2)}) collective-permute-start(bf16[2,384,128]{2,1,0:T(8,128)(2,1)S(1)} %collective-permute-done.2), channel_id=1, source_target_pairs={{0,240},{16,0},{32,16},{48,32},{64,48},{80,64},{96,80},{112,96},{1... | collective-permute-start | bytes 589832 | tf_op jit(solution)/shard_map/ppermute | solution.py:93
  176.6 5.3 %collective-permute-start.4 = (bf16[2,384,128]{2,1,0:T(8,128)(2,1)S(1)}, bf16[2,384,128]{2,1,0:T(8,128)(2,1)}, u32[]{:S(2)}, u32[]{:S(2)}) collective-permute-start(bf16[2,384,128]{2,1,0:T(8,128)(2,1)S(1)} %collective-permute-done.3), channel_id=1, source_target_pairs={{0,240},{16,0},{32,16},{48,32},{64,48},{80,64},{96,80},{112,96},{1... | collective-permute-start | bytes 589832 | tf_op jit(solution)/shard_map/ppermute | solution.py:93
  185.2 5.4 %collective-permute-start.5 = (bf16[2,384,128]{2,1,0:T(8,128)(2,1)}, bf16[2,384,128]{2,1,0:T(8,128)(2,1)S(1)}, u32[]{:S(2)}, u32[]{:S(2)}) collective-permute-start(bf16[2,384,128]{2,1,0:T(8,128)(2,1)} %collective-permute-done.4), channel_id=1, source_target_pairs={{0,240},{16,0},{32,16},{48,32},{64,48},{80,64},{96,80},{112,96},{1... | collective-permute-start | bytes 589832 | tf_op jit(solution)/shard_map/ppermute | solution.py:93
  194.2 4.6 %collective-permute-start.6 = (bf16[2,384,128]{2,1,0:T(8,128)(2,1)S(1)}, bf16[2,384,128]{2,1,0:T(8,128)(2,1)S(1)}, u32[]{:S(2)}, u32[]{:S(2)}) collective-permute-start(bf16[2,384,128]{2,1,0:T(8,128)(2,1)S(1)} %collective-permute-done.5), channel_id=1, source_target_pairs={{0,240},{16,0},{32,16},{48,32},{64,48},{80,64},{96,80},{112,96},{1... | collective-permute-start | bytes 589832 | tf_op jit(solution)/shard_map/ppermute | solution.py:93
  201.4 5.0 %collective-permute-done.13 = bf16[2,384,128]{2,1,0:T(8,128)(2,1)S(1)} collective-permute-done((bf16[2,384,128]{2,1,0:T(8,128)(2,1)S(1)}, bf16[2,384,128]{2,1,0:T(8,128)(2,1)S(1)}, u32[]{:S(2)}, u32[]{:S(2)}) %collective-permute-start.13) | collective-permute-done | bytes 196640 | tf_op jit(solution)/shard_map/ppermute | solution.py:90
  209.2 4.8 %collective-permute-done.14 = bf16[2,384,128]{2,1,0:T(8,128)(2,1)S(1)} collective-permute-done((bf16[2,384,128]{2,1,0:T(8,128)(2,1)S(1)}, bf16[2,384,128]{2,1,0:T(8,128)(2,1)S(1)}, u32[]{:S(2)}, u32[]{:S(2)}) %collective-permute-start.14) | collective-permute-done | bytes 196640 | tf_op jit(solution)/shard_map/ppermute | solution.py:90
  237.9 6.4 %fusion.28 = (f32[128]{0:T(128)S(1)}, bf16[128,2048]{1,0:T(8,128)(2,1)S(1)}) fusion(bf16[128,2048]{0,1:T(8,128)(2,1)S(1)} %bitcast.187, bf16[2048,2048]{0,1:T(8,128)(2,1)} %all-gather.3.cloned.1.call-done, bf16[128,2048]{1,0:T(8,128)(2,1)S(1)} %copy-done.1), kind=kOutput, calls=%fused_computation.32 | convolution fusion | flops 1075314560 | bytes 9961984 | tf_op jit(solution)/shard_map/dot_general | solution.py:161
  245.8 10.3 %all-to-all-start.4 = ((bf16[16,16,2048]{2,1,0:T(8,128)(2,1)}), bf16[16,16,2048]{2,1,0:T(8,128)(2,1)}, u32[]{:S(2)}, u32[]{:S(2)}) async-start(bf16[16,16,2048]{2,1,0:T(8,128)(2,1)} %bitcast.39), calls=%async_computation.4 | async-start | bytes 2097152 | tf_op jit(solution)/shard_map/all_to_all | solution.py:186
  267.0 4.6 %all-to-all-done.4 = bf16[16,16,2048]{2,1,0:T(8,128)(2,1)} async-done(((bf16[16,16,2048]{2,1,0:T(8,128)(2,1)}), bf16[16,16,2048]{2,1,0:T(8,128)(2,1)}, u32[]{:S(2)}, u32[]{:S(2)}) %all-to-all-start.4) | async-done | bytes 1048608 | tf_op jit(solution)/shard_map/all_to_all | solution.py:186
  273.6 3.8 %convolution_convert_fusion = bf16[16,16,2048]{2,1,0:T(8,128)(2,1)} fusion(bf16[256,2048,1]{0,1,2:T(8,128)(2,1)} %bitcast.192, bf16[16,16,2048]{2,1,0:T(8,128)(2,1)} %all-to-all-done.4, bf16[2048,256,1]{1,0,2:T(8,128)(2,1)S(1)} %reshape.274, f32[16,16,256]{2,1,0:T(8,128)S(1)} %fusion.67), kind=kOutput, calls=%fused_computation.21 | convolution fusion | flops 537788416 | bytes 4456448 | tf_op jit(solution)/shard_map/smp,pd->smd/dot_general | solution.py:190
  277.4 4.5 %all-to-all-start.5 = ((bf16[16,16,2048]{2,1,0:T(8,128)(2,1)}), bf16[16,16,2048]{2,1,0:T(8,128)(2,1)S(1)}, u32[]{:S(2)}, u32[]{:S(2)}) async-start(bf16[16,16,2048]{2,1,0:T(8,128)(2,1)} %convolution_convert_fusion), calls=%async_computation.5 | async-start | bytes 2097152 | tf_op jit(solution)/shard_map/all_to_all | solution.py:193
  282.0 15.5 %all-to-all-done.5 = bf16[16,16,2048]{2,1,0:T(8,128)(2,1)S(1)} async-done(((bf16[16,16,2048]{2,1,0:T(8,128)(2,1)}), bf16[16,16,2048]{2,1,0:T(8,128)(2,1)S(1)}, u32[]{:S(2)}, u32[]{:S(2)}) %all-to-all-start.5) | async-done | bytes 1048608 | tf_op jit(solution)/shard_map/all_to_all | solution.py:193
  (151 shorter events, 104.3 us)
Async XLA Ops:
  7.2 89.9 %copy-start.6 = (s32[128,8]{0,1:T(8,128)S(1)}, s32[128,8]{0,1:T(8,128)}, u32[]{:S(2)}) copy-start(s32[128,8]{0,1:T(8,128)} %param.26) | copy-start | bytes 12292
  7.2 89.9 %copy-start.4 = (bf16[128,2048]{1,0:T(8,128)(2,1)S(1)}, bf16[128,2048]{1,0:T(8,128)(2,1)}, u32[]{:S(2)}) copy-start(bf16[128,2048]{1,0:T(8,128)(2,1)} %param.16) | copy-start | bytes 1572868
  7.2 230.7 %all-gather.3.cloned.1.call-start = ((), (), s32[]{:S(2)}) async-start(), calls=%async_computation.6 | async-start | bytes 8912896 | tf_op jit(solution)/shard_map/all_gather | solution.py:163
  56.0 59.4 %collective-permute-start = (bf16[2,384,128]{2,1,0:T(8,128)(2,1)S(1)}, bf16[2,384,128]{2,1,0:T(8,128)(2,1)S(1)}, u32[]{:S(2)}, u32[]{:S(2)}) collective-permute-start(bf16[2,384,128]{2,1,0:T(8,128)(2,1)S(1)} %all_gather.19), channel_id=1, source_target_pairs={{0,240},{16,0},{32,16},{48,32},{64,48},{80,64},{96,80},{112,96},{1... | collective-permute-start | bytes 589832 | tf_op jit(solution)/shard_map/ppermute | solution.py:93
  57.9 61.0 %collective-permute-start.7 = (bf16[2,384,128]{2,1,0:T(8,128)(2,1)S(1)}, bf16[2,384,128]{2,1,0:T(8,128)(2,1)S(1)}, u32[]{:S(2)}, u32[]{:S(2)}) collective-permute-start(bf16[2,384,128]{2,1,0:T(8,128)(2,1)S(1)} %all_gather.19), channel_id=1, source_target_pairs={{0,16},{16,32},{32,48},{48,64},{64,80},{80,96},{96,112},{112,128},... | collective-permute-start | bytes 589832 | tf_op jit(solution)/shard_map/ppermute | solution.py:90
  62.2 29.8 %all-to-all-start.1 = ((bf16[128,16,128]{2,0,1:T(8,128)(2,1)}), bf16[128,16,128]{2,0,1:T(8,128)(2,1)S(1)}, u32[]{:S(2)}, u32[]{:S(2)}) async-start(bf16[128,16,128]{2,0,1:T(8,128)(2,1)} %copy_bitcast_fusion.2), calls=%async_computation.1 | async-start | bytes 1048576 | tf_op jit(solution)/shard_map/all_to_all | solution.py:118
  92.9 17.8 %all-to-all-start.2 = ((bf16[128,16,128]{2,0,1:T(8,128)(2,1)}), bf16[128,16,128]{2,0,1:T(8,128)(2,1)S(1)}, u32[]{:S(2)}, u32[]{:S(2)}) async-start(bf16[128,16,128]{2,0,1:T(8,128)(2,1)} %copy_bitcast_fusion.1), calls=%async_computation.2 | async-start | bytes 1048576 | tf_op jit(solution)/shard_map/all_to_all | solution.py:119
  110.7 33.0 %all-to-all-start = ((bf16[128,16,128]{0,2,1:T(8,128)(2,1)}), bf16[128,16,128]{0,2,1:T(8,128)(2,1)S(1)}, u32[]{:S(2)}, u32[]{:S(2)}) async-start(bf16[128,16,128]{0,2,1:T(8,128)(2,1)} %bitcast.10), calls=%async_computation | async-start | bytes 1048576 | tf_op jit(solution)/shard_map/all_to_all | solution.py:117
  115.3 8.3 %collective-permute-start.1 = (bf16[2,384,128]{2,1,0:T(8,128)(2,1)S(1)}, bf16[2,384,128]{2,1,0:T(8,128)(2,1)S(1)}, u32[]{:S(2)}, u32[]{:S(2)}) collective-permute-start(bf16[2,384,128]{2,1,0:T(8,128)(2,1)S(1)} %collective-permute-done), channel_id=1, source_target_pairs={{0,240},{16,0},{32,16},{48,32},{64,48},{80,64},{96,80},{112,96},{1... | collective-permute-start | bytes 589832 | tf_op jit(solution)/shard_map/ppermute | solution.py:93
  118.9 9.4 %collective-permute-start.8 = (bf16[2,384,128]{2,1,0:T(8,128)(2,1)S(1)}, bf16[2,384,128]{2,1,0:T(8,128)(2,1)S(1)}, u32[]{:S(2)}, u32[]{:S(2)}) collective-permute-start(bf16[2,384,128]{2,1,0:T(8,128)(2,1)S(1)} %collective-permute-done.7), channel_id=1, source_target_pairs={{0,16},{16,32},{32,48},{48,64},{64,80},{80,96},{96,112},{112,128},... | collective-permute-start | bytes 589832 | tf_op jit(solution)/shard_map/ppermute | solution.py:90
  123.7 44.0 %collective-permute-start.2 = (bf16[2,384,128]{2,1,0:T(8,128)(2,1)S(1)}, bf16[2,384,128]{2,1,0:T(8,128)(2,1)S(1)}, u32[]{:S(2)}, u32[]{:S(2)}) collective-permute-start(bf16[2,384,128]{2,1,0:T(8,128)(2,1)S(1)} %collective-permute-done.1), channel_id=1, source_target_pairs={{0,240},{16,0},{32,16},{48,32},{64,48},{80,64},{96,80},{112,96},{1... | collective-permute-start | bytes 589832 | tf_op jit(solution)/shard_map/ppermute | solution.py:93
  128.4 44.1 %collective-permute-start.9 = (bf16[2,384,128]{2,1,0:T(8,128)(2,1)S(1)}, bf16[2,384,128]{2,1,0:T(8,128)(2,1)S(1)}, u32[]{:S(2)}, u32[]{:S(2)}) collective-permute-start(bf16[2,384,128]{2,1,0:T(8,128)(2,1)S(1)} %collective-permute-done.8), channel_id=1, source_target_pairs={{0,16},{16,32},{32,48},{48,64},{64,80},{80,96},{96,112},{112,128},... | collective-permute-start | bytes 589832 | tf_op jit(solution)/shard_map/ppermute | solution.py:90
  160.3 24.2 %all-to-all-start.3 = ((bf16[16,128,128]{2,1,0:T(8,128)(2,1)}), bf16[16,128,128]{2,1,0:T(8,128)(2,1)S(1)}, u32[]{:S(2)}, u32[]{:S(2)}) async-start(bf16[16,128,128]{2,1,0:T(8,128)(2,1)} %bitcast.31), calls=%async_computation.3 | async-start | bytes 1048576 | tf_op jit(solution)/shard_map/all_to_all | solution.py:141
  167.6 9.0 %collective-permute-start.3 = (bf16[2,384,128]{2,1,0:T(8,128)(2,1)S(1)}, bf16[2,384,128]{2,1,0:T(8,128)(2,1)S(1)}, u32[]{:S(2)}, u32[]{:S(2)}) collective-permute-start(bf16[2,384,128]{2,1,0:T(8,128)(2,1)S(1)} %collective-permute-done.2), channel_id=1, source_target_pairs={{0,240},{16,0},{32,16},{48,32},{64,48},{80,64},{96,80},{112,96},{1... | collective-permute-start | bytes 589832 | tf_op jit(solution)/shard_map/ppermute | solution.py:93
  172.5 9.4 %collective-permute-start.10 = (bf16[2,384,128]{2,1,0:T(8,128)(2,1)S(1)}, bf16[2,384,128]{2,1,0:T(8,128)(2,1)S(1)}, u32[]{:S(2)}, u32[]{:S(2)}) collective-permute-start(bf16[2,384,128]{2,1,0:T(8,128)(2,1)S(1)} %collective-permute-done.9), channel_id=1, source_target_pairs={{0,16},{16,32},{32,48},{48,64},{64,80},{80,96},{96,112},{112,128},... | collective-permute-start | bytes 589832 | tf_op jit(solution)/shard_map/ppermute | solution.py:90
  176.6 8.6 %collective-permute-start.4 = (bf16[2,384,128]{2,1,0:T(8,128)(2,1)S(1)}, bf16[2,384,128]{2,1,0:T(8,128)(2,1)}, u32[]{:S(2)}, u32[]{:S(2)}) collective-permute-start(bf16[2,384,128]{2,1,0:T(8,128)(2,1)S(1)} %collective-permute-done.3), channel_id=1, source_target_pairs={{0,240},{16,0},{32,16},{48,32},{64,48},{80,64},{96,80},{112,96},{1... | collective-permute-start | bytes 589832 | tf_op jit(solution)/shard_map/ppermute | solution.py:93
  181.9 8.7 %collective-permute-start.11 = (bf16[2,384,128]{2,1,0:T(8,128)(2,1)S(1)}, bf16[2,384,128]{2,1,0:T(8,128)(2,1)S(1)}, u32[]{:S(2)}, u32[]{:S(2)}) collective-permute-start(bf16[2,384,128]{2,1,0:T(8,128)(2,1)S(1)} %collective-permute-done.10), channel_id=1, source_target_pairs={{0,16},{16,32},{32,48},{48,64},{64,80},{80,96},{96,112},{112,128},... | collective-permute-start | bytes 589832 | tf_op jit(solution)/shard_map/ppermute | solution.py:90
  185.2 9.0 %collective-permute-start.5 = (bf16[2,384,128]{2,1,0:T(8,128)(2,1)}, bf16[2,384,128]{2,1,0:T(8,128)(2,1)S(1)}, u32[]{:S(2)}, u32[]{:S(2)}) collective-permute-start(bf16[2,384,128]{2,1,0:T(8,128)(2,1)} %collective-permute-done.4), channel_id=1, source_target_pairs={{0,240},{16,0},{32,16},{48,32},{64,48},{80,64},{96,80},{112,96},{1... | collective-permute-start | bytes 589832 | tf_op jit(solution)/shard_map/ppermute | solution.py:93
  190.6 8.1 %collective-permute-start.12 = (bf16[2,384,128]{2,1,0:T(8,128)(2,1)S(1)}, bf16[2,384,128]{2,1,0:T(8,128)(2,1)S(1)}, u32[]{:S(2)}, u32[]{:S(2)}) collective-permute-start(bf16[2,384,128]{2,1,0:T(8,128)(2,1)S(1)} %collective-permute-done.11), channel_id=1, source_target_pairs={{0,16},{16,32},{32,48},{48,64},{64,80},{80,96},{96,112},{112,128},... | collective-permute-start | bytes 589832 | tf_op jit(solution)/shard_map/ppermute | solution.py:90
  194.2 14.3 %collective-permute-start.6 = (bf16[2,384,128]{2,1,0:T(8,128)(2,1)S(1)}, bf16[2,384,128]{2,1,0:T(8,128)(2,1)S(1)}, u32[]{:S(2)}, u32[]{:S(2)}) collective-permute-start(bf16[2,384,128]{2,1,0:T(8,128)(2,1)S(1)} %collective-permute-done.5), channel_id=1, source_target_pairs={{0,240},{16,0},{32,16},{48,32},{64,48},{80,64},{96,80},{112,96},{1... | collective-permute-start | bytes 589832 | tf_op jit(solution)/shard_map/ppermute | solution.py:93
  198.8 7.6 %collective-permute-start.13 = (bf16[2,384,128]{2,1,0:T(8,128)(2,1)S(1)}, bf16[2,384,128]{2,1,0:T(8,128)(2,1)S(1)}, u32[]{:S(2)}, u32[]{:S(2)}) collective-permute-start(bf16[2,384,128]{2,1,0:T(8,128)(2,1)S(1)} %collective-permute-done.12), channel_id=1, source_target_pairs={{0,16},{16,32},{32,48},{48,64},{64,80},{80,96},{96,112},{112,128},... | collective-permute-start | bytes 589832 | tf_op jit(solution)/shard_map/ppermute | solution.py:90
  206.4 7.6 %collective-permute-start.14 = (bf16[2,384,128]{2,1,0:T(8,128)(2,1)S(1)}, bf16[2,384,128]{2,1,0:T(8,128)(2,1)S(1)}, u32[]{:S(2)}, u32[]{:S(2)}) collective-permute-start(bf16[2,384,128]{2,1,0:T(8,128)(2,1)S(1)} %collective-permute-done.13), channel_id=1, source_target_pairs={{0,16},{16,32},{32,48},{48,64},{64,80},{80,96},{96,112},{112,128},... | collective-permute-start | bytes 589832 | tf_op jit(solution)/shard_map/ppermute | solution.py:90
  245.8 25.8 %all-to-all-start.4 = ((bf16[16,16,2048]{2,1,0:T(8,128)(2,1)}), bf16[16,16,2048]{2,1,0:T(8,128)(2,1)}, u32[]{:S(2)}, u32[]{:S(2)}) async-start(bf16[16,16,2048]{2,1,0:T(8,128)(2,1)} %bitcast.39), calls=%async_computation.4 | async-start | bytes 2097152 | tf_op jit(solution)/shard_map/all_to_all | solution.py:186
  277.4 20.1 %all-to-all-start.5 = ((bf16[16,16,2048]{2,1,0:T(8,128)(2,1)}), bf16[16,16,2048]{2,1,0:T(8,128)(2,1)S(1)}, u32[]{:S(2)}, u32[]{:S(2)}) async-start(bf16[16,16,2048]{2,1,0:T(8,128)(2,1)} %convolution_convert_fusion), calls=%async_computation.5 | async-start | bytes 2097152 | tf_op jit(solution)/shard_map/all_to_all | solution.py:193
  (9 other events, 311.1 us)
Sparse Core Ops, SparseCore 0:
  47.6 88.5 all-gather.2

commit v3 on v1

--- a/solution.py
+++ b/solution.py
@@ -63,19 +63,6 @@
         return output.astype(jnp.bfloat16).reshape(block_rows, heads_here * HD)
 
     return lax.map(one_block, (q_blocks, seg_blocks)).reshape(group_rows, heads_here * HD)
-
-
-def gather_dp(pieces):
-    flat = jnp.concatenate([p.reshape(-1) for p in pieces])
-    lanes = 128
-    packed = flat.reshape(-1, lanes)
-    gathered = lax.all_gather(lax.all_gather(packed, "dh"), "dz")
-    gathered = jnp.swapaxes(gathered, 0, 1).reshape(-1, flat.shape[0])
-    out, at = [], 0
-    for p in pieces:
-        out.append(gathered[:, at : at + p.size].reshape((-1,) + p.shape))
-        at += p.size
-    return out
 
 
 def body(
@@ -116,25 +103,32 @@
         .set(v_heads)
         .reshape(pool_size, PAGE, head_width)
     )
+    pieces = [
+        wo_shard.astype(jnp.bfloat16).T,
+        gate_shard[0].astype(jnp.bfloat16),
+        up_shard[0].astype(jnp.bfloat16),
+        down_shard[0].astype(jnp.bfloat16),
+    ]
+    packed = jnp.concatenate([p.reshape(-1) for p in pieces]).reshape(-1, 128)
+    gathered = lax.all_gather(lax.all_gather(packed, "dh"), "dz")
+    gathered, q_heads, k_heads, v_heads, key_pages, value_pages = lax.optimization_barrier(
+        (gathered, q_heads, k_heads, v_heads, key_pages, value_pages)
+    )
+    wo_piece_rows = pieces[0].size // 128
+    wo_cols = jnp.swapaxes(gathered[:, :, :wo_piece_rows], 0, 1).reshape(-1, pieces[0].shape[1])
+    wo_full = lax.all_gather(wo_cols, "tensor", axis=1, tiled=True)
+    experts = jnp.swapaxes(gathered[:, :, wo_piece_rows:], 0, 1)
+    experts = experts.reshape(experts.shape[0] * experts.shape[1], -1)
+    weights_full, at = [], 0
+    for p in pieces[1:]:
+        weights_full.append(experts[:, at : at + p.size].reshape((-1,) + p.shape))
+        at += p.size
+    gate_full = weights_full[0].reshape(1, -1, gate_shard.shape[2])
+    up_full = weights_full[1].reshape(1, -1, up_shard.shape[2])
+    down_full = weights_full[2].transpose(1, 0, 2).reshape(1, down_shard.shape[1], -1)
     attended = attend_group(q_heads, k_heads, v_heads, segment, heads_here)
     token_rows = lax.all_to_all(attended, "tensor", split_axis=0, concat_axis=1, tiled=True)
-    weights_full = gather_dp(
-        [
-            wo_shard.astype(jnp.bfloat16),
-            gate_shard[0].astype(jnp.bfloat16),
-            up_shard[0].astype(jnp.bfloat16),
-            down_shard[0].astype(jnp.bfloat16),
-        ]
-    )
-    wo_rows = weights_full[0].transpose(1, 0, 2).reshape(wo_shard.shape[0], -1)
-    gate_full = weights_full[1].reshape(1, -1, gate_shard.shape[2])
-    up_full = weights_full[2].reshape(1, -1, up_shard.shape[2])
-    down_full = weights_full[3].transpose(1, 0, 2).reshape(1, down_shard.shape[1], -1)
-    projected = jnp.dot(
-        token_rows,
-        lax.all_gather(wo_rows, "tensor", axis=0, tiled=True),
-        preferred_element_type=jnp.float32,
-    )
+    projected = jnp.einsum("tr,cr->tc", token_rows, wo_full, preferred_element_type=jnp.float32)
     hidden_mid = (residual.astype(jnp.float32) + projected).astype(jnp.bfloat16)
     mid_float = hidden_mid.astype(jnp.float32)
     normed = (

time: 257 us -> 238 us (0.926)
  waiting for transfers between devices: 128 us -> 102 us
  starting transfers between devices: 37.5 us -> 43.5 us
    all_gather x2, waiting for transfers between devices: 76 us -> 60.5 us  [the longest x1 40.1 us: body(): wo_full = lax.all_gather(wo_cols, 'tensor', axis=1, tiled=True)]
    all_to_all x1, waiting for transfers between devices: 1.96 us -> 15.5 us  [body(): lax.all_to_all(result, 'tensor', split_axis=0, concat_axis=0, tiled=True)]
    all_to_all x1, waiting for transfers between devices: 12.4 us -> 0.01 us  [body(): lax.all_to_all(queries, 'tensor', split_axis=1, concat_axis=0, tiled=True)]
    all_to_all x1, starting transfers between devices: 4.48 us -> 14.8 us  [body(): lax.all_to_all(attended, 'tensor', split_axis=0, concat_axis=1, tiled=True)]
    all_to_all x1, waiting for transfers between devices: 10.6 us -> 5.7 us  [body(): lax.all_to_all(attended, 'tensor', split_axis=0, concat_axis=1, tiled=True)]
    all_to_all x1, starting transfers between devices: 15.2 us -> 10.6 us  [body(): lax.all_to_all(new_keys, 'tensor', split_axis=1, concat_axis=0, tiled=True)]
    all_to_all x1, waiting for transfers between devices: 13.2 us -> 8.68 us  [body(): lax.all_to_all(new_values, 'tensor', split_axis=1, concat_axis=0, tiled=T...]
    unnamed x32 -> x19, local copies, waits for them, and re-layouts: 7.32 us -> 3.88 us
  transfers between devices with their start and end apart: 8 -> 8, of which waited for: 8 -> 7; matrix products, arithmetic and copies ran while one was open for 16% -> 21% of each run, Pallas kernels for 0% -> 0%
where the time goes in v3:
time: 238 us; the launch traced here: 236 us
  waiting for transfers between devices  102 us (43%)
  starting transfers between devices  43.5 us (18%)
  local copies, waits for them, and re-layouts  37.5 us (16%)
  matrix products  24 us (10%)
  between operations  14.3 us (6%)
  other arithmetic  8.66 us (4%)
  blocking collectives  6.67 us (3%)
    all_gather x1, waiting for transfers between devices, body(): wo_full = lax.all_gather(wo_cols, 'tensor', axis=1, tiled=True)  40.1 us
    all_gather x1, waiting for transfers between devices, body(): gathered = lax.all_gather(lax.all_gather(packed, 'dh'), 'dz')  20.5 us
    all_to_all x1, waiting for transfers between devices, body(): lax.all_to_all(result, 'tensor', split_axis=0, concat_axis=0, tiled=True)  15.5 us
    all_to_all x1, starting transfers between devices, body(): lax.all_to_all(attended, 'tensor', split_axis=0, concat_axis=1, tiled=True)  14.8 us
    all_to_all x1, starting transfers between devices, body(): lax.all_to_all(new_keys, 'tensor', split_axis=1, concat_axis=0, tiled=True)  10.6 us
    all_to_all x1, waiting for transfers between devices, body(): lax.all_to_all(new_values, 'tensor', split_axis=1, concat_axis=0, tiled=T...  8.68 us
    all_gather x1, blocking collectives, body(): gathered = lax.all_gather(lax.all_gather(packed, 'dh'), 'dz')  6.67 us
    scatter x1, local copies, waits for them, and re-layouts, body(): value_pages = jnp.zeros((pool_size * PAGE, head_width), jnp.bfloat16).at[...  6.54 us
  transfers between devices with their start and end apart: 8, of which 7 were waited for; matrix products, arithmetic and copies ran while one was open for 21% of the time, Pallas kernels for 0%

profile of v3, /device:TPU:1, one launch (start us, length us, event | category | flops | bytes accessed | tf_op | source)
XLA Modules:
  0.0 236.3 jit_solution(14341236253968236352)
XLA Ops:
  10.9 6.7 %all_gather.12 = bf16[2,448,128]{2,1,0:T(8,128)(2,1)} all-gather(bf16[1,448,128]{2,1,0:T(8,128)(2,1)S(1)} %maximum_bitcast_fusion), channel_id=1, replica_groups=mesh['dh'=2,'dz'=16,'tensor'=16] {'dh'}, dimensions={0}, use_global_device_ids=true | all-gather | bytes 344064 | tf_op jit(solution)/shard_map/all_gather | solution.py:113
  18.6 10.6 %all-to-all-start.1 = ((bf16[128,16,128]{2,0,1:T(8,128)(2,1)}), bf16[128,16,128]{2,0,1:T(8,128)(2,1)S(1)}, u32[]{:S(2)}, u32[]{:S(2)}) async-start(bf16[128,16,128]{2,0,1:T(8,128)(2,1)} %copy_bitcast_fusion.2), calls=%async_computation.1 | async-start | bytes 1048576 | tf_op jit(solution)/shard_map/all_to_all | solution.py:87
  33.0 5.9 %all-to-all-done.1 = bf16[128,16,128]{2,0,1:T(8,128)(2,1)S(1)} async-done(((bf16[128,16,128]{2,0,1:T(8,128)(2,1)}), bf16[128,16,128]{2,0,1:T(8,128)(2,1)S(1)}, u32[]{:S(2)}, u32[]{:S(2)}) %all-to-all-start.1) | async-done | bytes 524320 | tf_op jit(solution)/shard_map/all_to_all | solution.py:87
  38.9 4.6 %all-to-all-start.2 = ((bf16[128,16,128]{2,0,1:T(8,128)(2,1)}), bf16[128,16,128]{2,0,1:T(8,128)(2,1)S(1)}, u32[]{:S(2)}, u32[]{:S(2)}) async-start(bf16[128,16,128]{2,0,1:T(8,128)(2,1)} %copy_bitcast_fusion.1), calls=%async_computation.2 | async-start | bytes 1048576 | tf_op jit(solution)/shard_map/all_to_all | solution.py:88
  44.6 8.7 %all-to-all-done.2 = bf16[128,16,128]{2,0,1:T(8,128)(2,1)S(1)} async-done(((bf16[128,16,128]{2,0,1:T(8,128)(2,1)}), bf16[128,16,128]{2,0,1:T(8,128)(2,1)S(1)}, u32[]{:S(2)}, u32[]{:S(2)}) %all-to-all-start.2) | async-done | bytes 524320 | tf_op jit(solution)/shard_map/all_to_all | solution.py:88
  53.3 4.6 %all-to-all-start = ((bf16[128,16,128]{2,0,1:T(8,128)(2,1)}), bf16[128,16,128]{2,0,1:T(8,128)(2,1)S(1)}, u32[]{:S(2)}, u32[]{:S(2)}) async-start(bf16[128,16,128]{2,0,1:T(8,128)(2,1)} %copy_bitcast_fusion.3), calls=%async_computation | async-start | bytes 1048576 | tf_op jit(solution)/shard_map/all_to_all | solution.py:86
  58.0 6.5 %scatter_custom_fusion.1 = bf16[2176,128]{1,0:T(8,128)(2,1)} fusion(s32[2048]{0:T(1024)S(1)} %bitcast.161, bf16[2048,128]{1,0:T(8,128)(2,1)S(1)} %bitcast.140, bf16[]{:T(256)} %constant.81.clone.1), kind=kCustom, calls=%fused_computation.42 | custom fusion | bytes 557058 | tf_op jit(solution)/shard_map/scatter | solution.py:103
  64.6 6.5 %scatter_custom_fusion = bf16[2176,128]{1,0:T(8,128)(2,1)} fusion(s32[2048]{0:T(1024)S(1)} %bitcast.162, bf16[2048,128]{1,0:T(8,128)(2,1)S(1)} %bitcast.153, bf16[]{:T(256)} %constant.81.clone.1), kind=kCustom, calls=%fused_computation.44 | custom fusion | bytes 557058 | tf_op jit(solution)/shard_map/scatter | solution.py:97
  71.1 20.5 %all-gather.6.cloned.1.call-done = bf16[32,448,128]{2,1,0:T(8,128)(2,1)} async-done(((bf16[2,448,128]{2,1,0:T(8,128)(2,1)}), bf16[32,448,128]{2,1,0:T(8,128)(2,1)}) %all-gather.6.cloned.1.call-update) | async-done | bytes 3670032 | tf_op jit(solution)/shard_map/all_gather | solution.py:113
  93.9 12.2 %while.10 = (s32[]{:T(128)}, bf16[4,512,128]{2,1,0:T(8,128)(2,1)}, s32[4,512]{1,0:T(4,128)S(1)}, s32[2048]{0:T(1024)S(1)}, bf16[4,512,1,128]{3,1,2,0:T(8,128)(2,...) while((s32[]{:T(128)}, bf16[4,512,128]{2,1,0:T(8,128)(2,1)}, ...), condition=%wide.region_11.12_spmd, body=%wide.region_8.11_spmd.sunk | while | flops 545389568 | bytes 13918313 | solution.py:65
  106.1 14.8 %all-to-all-start.3 = ((bf16[16,128,128]{2,1,0:T(8,128)(2,1)}), bf16[16,128,128]{2,1,0:T(8,128)(2,1)S(1)}, u32[]{:S(2)}, u32[]{:S(2)}) async-start(bf16[16,128,128]{2,1,0:T(8,128)(2,1)} %bitcast.35), calls=%async_computation.3 | async-start | bytes 1048576 | tf_op jit(solution)/shard_map/all_to_all | solution.py:130
  120.9 2.2 slice_bitcast_fusion
  123.5 3.8 %copy.88 = bf16[4,8,384,128]{3,1,2,0:T(8,128)(2,1)} copy(bf16[4,8,384,128]{3,2,1,0:T(8,128)(2,1)S(1)} %bitcast.143) | data formatting | bytes 6291456
  127.3 5.7 %all-to-all-done.3 = bf16[16,128,128]{2,1,0:T(8,128)(2,1)S(1)} async-done(((bf16[16,128,128]{2,1,0:T(8,128)(2,1)}), bf16[16,128,128]{2,1,0:T(8,128)(2,1)S(1)}, u32[]{:S(2)}, u32[]{:S(2)}) %all-to-all-start.3) | async-done | bytes 524320 | tf_op jit(solution)/shard_map/all_to_all | solution.py:130
  133.3 40.1 %all-gather.4.cloned.1.call-done = bf16[2048,2048]{1,0:T(8,128)(2,1)} async-done(((bf16[2048,128]{1,0:T(8,128)(2,1)}), bf16[2048,2048]{1,0:T(8,128)(2,1)}) %all-gather.4.cloned.1.call-update) | async-done | bytes 8388624 | tf_op jit(solution)/shard_map/all_gather | solution.py:119
  173.4 6.4 %fusion.28 = (f32[128]{0:T(128)S(1)}, bf16[128,2048]{1,0:T(8,128)(2,1)S(1)}) fusion(bf16[128,2048]{0,1:T(8,128)(2,1)S(1)} %bitcast.147, bf16[2048,2048]{1,0:T(8,128)(2,1)} %all-gather.4.cloned.1.call-done, bf16[128,2048]{1,0:T(8,128)(2,1)S(1)} %copy-done.1), kind=kOutput, calls=%fused_computation.32 | convolution fusion | flops 1075314560 | bytes 9961984 | tf_op jit(solution)/shard_map/tr,cr->tc/dot_general | solution.py:131
  181.3 4.3 %all-to-all-start.4 = ((bf16[16,16,2048]{2,1,0:T(8,128)(2,1)}), bf16[16,16,2048]{2,1,0:T(8,128)(2,1)}, u32[]{:S(2)}, u32[]{:S(2)}) async-start(bf16[16,16,2048]{2,1,0:T(8,128)(2,1)} %bitcast.41), calls=%async_computation.4 | async-start | bytes 2097152 | tf_op jit(solution)/shard_map/all_to_all | solution.py:152
  185.6 3.0 %fusion.66 = (bf16[32,16384]{1,0:T(8,128)(2,1)S(1)}, bf16[32,16384]{1,0:T(8,128)(2,1)}, bf16[32,16384]{1,0:T(8,128)(2,1)S(1)}) fusion(bf16[32,49152]{1,0:T(8,128)(2,1)} %bitcast.142), kind=kLoop, calls=%fused_computation.103 | loop fusion | bytes 6291456 | tf_op jit(solution)/shard_map/slice | solution.py:124
  191.3 3.0 %reshape.256 = bf16[32,256,64]{2,1,0:T(8,128)(2,1)S(1)} reshape(bf16[32,16384]{1,0:T(8,128)(2,1)} %get-tuple-element.101) | data formatting | bytes 2097152 | tf_op jit(solution)/shard_map/reshape | solution.py:124
  195.9 5.3 %all-to-all-done.4 = bf16[16,16,2048]{2,1,0:T(8,128)(2,1)} async-done(((bf16[16,16,2048]{2,1,0:T(8,128)(2,1)}), bf16[16,16,2048]{2,1,0:T(8,128)(2,1)}, u32[]{:S(2)}, u32[]{:S(2)}) %all-to-all-start.4) | async-done | bytes 1048608 | tf_op jit(solution)/shard_map/all_to_all | solution.py:152
  201.3 2.0 fusion.67
  203.3 4.2 %convolution_convert_fusion = bf16[16,16,2048]{2,1,0:T(8,128)(2,1)} fusion(bf16[256,2048,1]{0,1,2:T(8,128)(2,1)} %bitcast.150, bf16[16,16,2048]{2,1,0:T(8,128)(2,1)} %all-to-all-done.4, bf16[2048,256,1]{1,0,2:T(8,128)(2,1)} %reshape.277, f32[16,16,256]{2,1,0:T(8,128)S(1)} %fusion.67), kind=kOutput, calls=%fused_computation.21 | convolution fusion | flops 537788416 | bytes 4456448 | tf_op jit(solution)/shard_map/smp,pd->smd/dot_general | solution.py:156
  207.4 4.5 %all-to-all-start.5 = ((bf16[16,16,2048]{2,1,0:T(8,128)(2,1)}), bf16[16,16,2048]{2,1,0:T(8,128)(2,1)S(1)}, u32[]{:S(2)}, u32[]{:S(2)}) async-start(bf16[16,16,2048]{2,1,0:T(8,128)(2,1)} %convolution_convert_fusion), calls=%async_computation.5 | async-start | bytes 2097152 | tf_op jit(solution)/shard_map/all_to_all | solution.py:159
  212.0 15.5 %all-to-all-done.5 = bf16[16,16,2048]{2,1,0:T(8,128)(2,1)S(1)} async-done(((bf16[16,16,2048]{2,1,0:T(8,128)(2,1)}), bf16[16,16,2048]{2,1,0:T(8,128)(2,1)S(1)}, u32[]{:S(2)}, u32[]{:S(2)}) %all-to-all-start.5) | async-done | bytes 1048608 | tf_op jit(solution)/shard_map/all_to_all | solution.py:159
  (80 shorter events, 32.6 us)
Async XLA Ops:
  7.2 10.5 %copy-start = (bf16[128,2048]{1,0:T(8,128)(2,1)S(1)}, bf16[128,2048]{1,0:T(8,128)(2,1)}, u32[]{:S(2)}) copy-start(bf16[128,2048]{1,0:T(8,128)(2,1)} %param.17) | copy-start | bytes 1572868
  7.2 36.4 %copy-start.6 = (s32[1,17]{1,0:T(1,128)S(1)}, s32[1,17]{1,0:T(1,128)}, u32[]{:S(2)}) copy-start(s32[1,17]{1,0:T(1,128)} %param.20) | copy-start | bytes 208
  7.2 36.5 %copy-start.3 = (bf16[128,2048]{1,0:T(8,128)(2,1)S(1)}, bf16[128,2048]{1,0:T(8,128)(2,1)}, u32[]{:S(2)}) copy-start(bf16[128,2048]{1,0:T(8,128)(2,1)} %param.16) | copy-start | bytes 1572868
  7.2 84.4 %all-gather.6.cloned.1.call-start = ((), (), s32[]{:S(2)}) async-start(), calls=%async_computation.7 | async-start | bytes 3899392 | tf_op jit(solution)/shard_map/all_gather | solution.py:113
  18.6 20.4 %all-to-all-start.1 = ((bf16[128,16,128]{2,0,1:T(8,128)(2,1)}), bf16[128,16,128]{2,0,1:T(8,128)(2,1)S(1)}, u32[]{:S(2)}, u32[]{:S(2)}) async-start(bf16[128,16,128]{2,0,1:T(8,128)(2,1)} %copy_bitcast_fusion.2), calls=%async_computation.1 | async-start | bytes 1048576 | tf_op jit(solution)/shard_map/all_to_all | solution.py:87
  29.2 64.4 %copy-start.4 = (s32[128,8]{0,1:T(8,128)S(1)}, s32[128,8]{0,1:T(8,128)}, u32[]{:S(2)}) copy-start(s32[128,8]{0,1:T(8,128)} %param.26) | copy-start | bytes 12292
  38.9 14.4 %all-to-all-start.2 = ((bf16[128,16,128]{2,0,1:T(8,128)(2,1)}), bf16[128,16,128]{2,0,1:T(8,128)(2,1)S(1)}, u32[]{:S(2)}, u32[]{:S(2)}) async-start(bf16[128,16,128]{2,0,1:T(8,128)(2,1)} %copy_bitcast_fusion.1), calls=%async_computation.2 | async-start | bytes 1048576 | tf_op jit(solution)/shard_map/all_to_all | solution.py:88
  53.3 17.8 %all-to-all-start = ((bf16[128,16,128]{2,0,1:T(8,128)(2,1)}), bf16[128,16,128]{2,0,1:T(8,128)(2,1)S(1)}, u32[]{:S(2)}, u32[]{:S(2)}) async-start(bf16[128,16,128]{2,0,1:T(8,128)(2,1)} %copy_bitcast_fusion.3), calls=%async_computation | async-start | bytes 1048576 | tf_op jit(solution)/shard_map/all_to_all | solution.py:86
  57.9 115.4 %all-gather.4.cloned.1.call-start = ((), (), s32[]{:S(2)}) async-start(), calls=%async_computation.6 | async-start | bytes 8912896 | tf_op jit(solution)/shard_map/all_gather | solution.py:119
  106.1 27.0 %all-to-all-start.3 = ((bf16[16,128,128]{2,1,0:T(8,128)(2,1)}), bf16[16,128,128]{2,1,0:T(8,128)(2,1)S(1)}, u32[]{:S(2)}, u32[]{:S(2)}) async-start(bf16[16,128,128]{2,1,0:T(8,128)(2,1)} %bitcast.35), calls=%async_computation.3 | async-start | bytes 1048576 | tf_op jit(solution)/shard_map/all_to_all | solution.py:130
  123.5 49.8 %copy-start.1 = (bf16[128,2048]{1,0:T(8,128)(2,1)S(1)}, bf16[128,2048]{1,0:T(8,128)(2,1)}, u32[]{:S(2)}) copy-start(bf16[128,2048]{1,0:T(8,128)(2,1)} %param.15) | copy-start | bytes 1572868
  173.4 6.4 %copy-start.7 = (f32[2048]{0:T(1024)S(1)}, f32[2048]{0:T(1024)}, u32[]{:S(2)}) copy-start(f32[2048]{0:T(1024)} %param.22) | copy-start | bytes 24580
  179.7 8.9 %copy-start.2 = (bf16[128,2048]{1,0:T(8,128)(2,1)}, bf16[128,2048]{1,0:T(8,128)(2,1)S(1)}, u32[]{:S(2)}) copy-start(bf16[128,2048]{1,0:T(8,128)(2,1)S(1)} %get-tuple-element.106) | copy-start | bytes 1572868
  181.3 20.0 %all-to-all-start.4 = ((bf16[16,16,2048]{2,1,0:T(8,128)(2,1)}), bf16[16,16,2048]{2,1,0:T(8,128)(2,1)}, u32[]{:S(2)}, u32[]{:S(2)}) async-start(bf16[16,16,2048]{2,1,0:T(8,128)(2,1)} %bitcast.41), calls=%async_computation.4 | async-start | bytes 2097152 | tf_op jit(solution)/shard_map/all_to_all | solution.py:152
  195.9 16.0 %copy-start.5 = (f32[128,8]{0,1:T(8,128)S(1)}, f32[128,8]{0,1:T(8,128)}, u32[]{:S(2)}) copy-start(f32[128,8]{0,1:T(8,128)} %param.27) | copy-start | bytes 12292
  207.4 20.1 %all-to-all-start.5 = ((bf16[16,16,2048]{2,1,0:T(8,128)(2,1)}), bf16[16,16,2048]{2,1,0:T(8,128)(2,1)S(1)}, u32[]{:S(2)}, u32[]{:S(2)}) async-start(bf16[16,16,2048]{2,1,0:T(8,128)(2,1)} %convolution_convert_fusion), calls=%async_computation.5 | async-start | bytes 2097152 | tf_op jit(solution)/shard_map/all_to_all | solution.py:159
Sparse Core Ops, SparseCore 0:
  17.7 73.7 all-gather.5
  94.2 79.1 all-gather.3

commit v4 on v3

--- a/solution.py
+++ b/solution.py
@@ -103,13 +103,8 @@
         .set(v_heads)
         .reshape(pool_size, PAGE, head_width)
     )
-    pieces = [
-        wo_shard.astype(jnp.bfloat16).T,
-        gate_shard[0].astype(jnp.bfloat16),
-        up_shard[0].astype(jnp.bfloat16),
-        down_shard[0].astype(jnp.bfloat16),
-    ]
-    packed = jnp.concatenate([p.reshape(-1) for p in pieces]).reshape(-1, 128)
+    pieces = [wo_shard.T, gate_shard[0], up_shard[0], down_shard[0]]
+    packed = jnp.concatenate([p.reshape(-1) for p in pieces]).astype(jnp.bfloat16).reshape(-1, 128)
     gathered = lax.all_gather(lax.all_gather(packed, "dh"), "dz")
     gathered, q_heads, k_heads, v_heads, key_pages, value_pages = lax.optimization_barrier(
         (gathered, q_heads, k_heads, v_heads, key_pages, value_pages)
@@ -127,6 +122,9 @@
     up_full = weights_full[1].reshape(1, -1, up_shard.shape[2])
     down_full = weights_full[2].transpose(1, 0, 2).reshape(1, down_shard.shape[1], -1)
     attended = attend_group(q_heads, k_heads, v_heads, segment, heads_here)
+    attended, gate_full, up_full, down_full = lax.optimization_barrier(
+        (attended, gate_full, up_full, down_full)
+    )
     token_rows = lax.all_to_all(attended, "tensor", split_axis=0, concat_axis=1, tiled=True)
     projected = jnp.einsum("tr,cr->tc", token_rows, wo_full, preferred_element_type=jnp.float32)
     hidden_mid = (residual.astype(jnp.float32) + projected).astype(jnp.bfloat16)

time: 238 us -> 239 us (level)
  blocking collectives: 6.67 us -> 26.3 us
  waiting for transfers between devices: 102 us -> 88 us
  starting transfers between devices: 43.5 us -> 39.4 us
  local copies, waits for them, and re-layouts: 37.5 us -> 35.1 us
    all_to_all x0 -> x1, blocking collectives: none -> 19.6 us  [body(): lax.all_to_all(outgoing, 'tensor', split_axis=0, concat_axis=0, tiled=True)]
    all_gather x1, waiting for transfers between devices: 40.1 us -> 24.2 us  [body(): wo_full = lax.all_gather(wo_cols, 'tensor', axis=1, tiled=True)]
    all_to_all x1, waiting for transfers between devices: 5.7 us -> 13.3 us  [body(): lax.all_to_all(attended, 'tensor', split_axis=0, concat_axis=1, tiled=True)]
    all_to_all x1 -> x0, waiting for transfers between devices: 5.34 us -> none  [body(): lax.all_to_all(outgoing, 'tensor', split_axis=0, concat_axis=0, tiled=True)]
    all_to_all x1 -> x0, starting transfers between devices: 4.32 us -> none  [body(): lax.all_to_all(outgoing, 'tensor', split_axis=0, concat_axis=0, tiled=True)]
    dot_general x4, matrix products: 3.53 us -> 7.13 us  [one_block(): jnp.einsum('qhd,khd->hqk', q_block, k_split, preferred_element_type=jnp.f...]
  transfers between devices with their start and end apart: 8 -> 7, of which waited for: 7 -> 6; matrix products, arithmetic and copies ran while one was open for 21% -> 21% of each run, Pallas kernels for 0% -> 0%
where the time goes in v4:
time: 239 us; the launch traced here: 238 us
  waiting for transfers between devices  88 us (37%)
  starting transfers between devices  39.4 us (16%)
  local copies, waits for them, and re-layouts  35.1 us (15%)
  blocking collectives  26.3 us (11%)
  matrix products  25.7 us (11%)
  between operations  14.3 us (6%)
  other arithmetic  8.66 us (4%)
    all_gather x1, waiting for transfers between devices, body(): wo_full = lax.all_gather(wo_cols, 'tensor', axis=1, tiled=True)  24.2 us
    all_gather x1, waiting for transfers between devices, body(): gathered = lax.all_gather(lax.all_gather(packed, 'dh'), 'dz')  20.4 us
    all_to_all x1, blocking collectives, body(): lax.all_to_all(outgoing, 'tensor', split_axis=0, concat_axis=0, tiled=True)  19.6 us
    all_to_all x1, waiting for transfers between devices, body(): lax.all_to_all(result, 'tensor', split_axis=0, concat_axis=0, tiled=True)  15.5 us
    all_to_all x1, starting transfers between devices, body(): lax.all_to_all(attended, 'tensor', split_axis=0, concat_axis=1, tiled=True)  14.8 us
    all_to_all x1, waiting for transfers between devices, body(): lax.all_to_all(attended, 'tensor', split_axis=0, concat_axis=1, tiled=True)  13.3 us
    all_to_all x1, starting transfers between devices, body(): lax.all_to_all(new_keys, 'tensor', split_axis=1, concat_axis=0, tiled=True)  10.6 us
    all_to_all x1, waiting for transfers between devices, body(): lax.all_to_all(new_values, 'tensor', split_axis=1, concat_axis=0, tiled=T...  8.68 us
  transfers between devices with their start and end apart: 7, of which 6 were waited for; matrix products, arithmetic and copies ran while one was open for 21% of the time, Pallas kernels for 0%

profile of v4, /device:TPU:1, one launch (start us, length us, event | category | flops | bytes accessed | tf_op | source)
XLA Modules:
  0.0 237.6 jit_solution(7400599723608161134)
XLA Ops:
  10.9 6.7 %all_gather.12 = bf16[2,448,128]{2,1,0:T(8,128)(2,1)} all-gather(bf16[1,448,128]{2,1,0:T(8,128)(2,1)S(1)} %maximum_bitcast_fusion), channel_id=1, replica_groups=mesh['dh'=2,'dz'=16,'tensor'=16] {'dh'}, dimensions={0}, use_global_device_ids=true | all-gather | bytes 344064 | tf_op jit(solution)/shard_map/all_gather | solution.py:108
  18.6 10.6 %all-to-all-start.1 = ((bf16[128,16,128]{2,0,1:T(8,128)(2,1)}), bf16[128,16,128]{2,0,1:T(8,128)(2,1)S(1)}, u32[]{:S(2)}, u32[]{:S(2)}) async-start(bf16[128,16,128]{2,0,1:T(8,128)(2,1)} %copy_bitcast_fusion.2), calls=%async_computation.1 | async-start | bytes 1048576 | tf_op jit(solution)/shard_map/all_to_all | solution.py:87
  31.0 2.0 copy_bitcast_fusion.1
  33.0 5.9 %all-to-all-done.1 = bf16[128,16,128]{2,0,1:T(8,128)(2,1)S(1)} async-done(((bf16[128,16,128]{2,0,1:T(8,128)(2,1)}), bf16[128,16,128]{2,0,1:T(8,128)(2,1)S(1)}, u32[]{:S(2)}, u32[]{:S(2)}) %all-to-all-start.1) | async-done | bytes 524320 | tf_op jit(solution)/shard_map/all_to_all | solution.py:87
  38.9 4.6 %all-to-all-start.2 = ((bf16[128,16,128]{2,0,1:T(8,128)(2,1)}), bf16[128,16,128]{2,0,1:T(8,128)(2,1)S(1)}, u32[]{:S(2)}, u32[]{:S(2)}) async-start(bf16[128,16,128]{2,0,1:T(8,128)(2,1)} %copy_bitcast_fusion.1), calls=%async_computation.2 | async-start | bytes 1048576 | tf_op jit(solution)/shard_map/all_to_all | solution.py:88
  44.6 8.7 %all-to-all-done.2 = bf16[128,16,128]{2,0,1:T(8,128)(2,1)S(1)} async-done(((bf16[128,16,128]{2,0,1:T(8,128)(2,1)}), bf16[128,16,128]{2,0,1:T(8,128)(2,1)S(1)}, u32[]{:S(2)}, u32[]{:S(2)}) %all-to-all-start.2) | async-done | bytes 524320 | tf_op jit(solution)/shard_map/all_to_all | solution.py:88
  53.3 4.6 %all-to-all-start = ((bf16[128,16,128]{2,0,1:T(8,128)(2,1)}), bf16[128,16,128]{2,0,1:T(8,128)(2,1)S(1)}, u32[]{:S(2)}, u32[]{:S(2)}) async-start(bf16[128,16,128]{2,0,1:T(8,128)(2,1)} %copy_bitcast_fusion.3), calls=%async_computation | async-start | bytes 1048576 | tf_op jit(solution)/shard_map/all_to_all | solution.py:86
  58.0 6.5 %scatter_custom_fusion = bf16[2176,128]{1,0:T(8,128)(2,1)} fusion(s32[2048]{0:T(1024)S(1)} %bitcast.170, bf16[2048,128]{1,0:T(8,128)(2,1)S(1)} %bitcast.162, bf16[]{:T(256)} %constant.81.clone.1), kind=kCustom, calls=%fused_computation.48 | custom fusion | bytes 557058 | tf_op jit(solution)/shard_map/scatter | solution.py:97
  64.6 6.5 %scatter_custom_fusion.1 = bf16[2176,128]{1,0:T(8,128)(2,1)} fusion(s32[2048]{0:T(1024)S(1)} %bitcast.171, bf16[2048,128]{1,0:T(8,128)(2,1)S(1)} %bitcast.148, bf16[]{:T(256)} %constant.81.clone.1), kind=kCustom, calls=%fused_computation.46 | custom fusion | bytes 557058 | tf_op jit(solution)/shard_map/scatter | solution.py:103
  71.1 20.4 %all-gather.6.cloned.1.call-done = bf16[32,448,128]{2,1,0:T(8,128)(2,1)} async-done(((bf16[2,448,128]{2,1,0:T(8,128)(2,1)}), bf16[32,448,128]{2,1,0:T(8,128)(2,1)}) %all-gather.6.cloned.1.call-update) | async-done | bytes 3670032 | tf_op jit(solution)/shard_map/all_gather | solution.py:108
  93.5 2.2 slice_bitcast_fusion
  96.1 2.0 copy.87
  98.1 1.8 fusion.71
  100.0 3.0 %reshape.262 = bf16[32,256,64]{2,1,0:T(8,128)(2,1)S(1)} reshape(bf16[32,16384]{1,0:T(8,128)(2,1)} %get-tuple-element.108) | data formatting | bytes 2097152 | tf_op jit(solution)/shard_map/reshape | solution.py:119
  106.3 2.3 reshape_reshape.7
  108.7 15.8 %while.10 = (s32[]{:T(128)}, bf16[4,512,128]{2,1,0:T(8,128)(2,1)}, s32[4,512]{1,0:T(4,128)S(1)}, s32[2048]{0:T(1024)S(1)}, bf16[4,512,1,128]{3,1,2,0:T(8,128)(2,...) while((s32[]{:T(128)}, bf16[4,512,128]{2,1,0:T(8,128)(2,1)}, ...), condition=%wide.region_11.12_spmd, body=%wide.region_8.11_spmd.sunk | while | flops 545389568 | bytes 13919321 | solution.py:65
  124.5 14.8 %all-to-all-start.3 = ((bf16[16,128,128]{2,1,0:T(8,128)(2,1)}), bf16[16,128,128]{2,1,0:T(8,128)(2,1)S(1)}, u32[]{:S(2)}, u32[]{:S(2)}) async-start(bf16[16,128,128]{2,1,0:T(8,128)(2,1)} %bitcast.39), calls=%async_computation.3 | async-start | bytes 1048576 | tf_op jit(solution)/shard_map/all_to_all | solution.py:128
  139.7 13.3 %all-to-all-done.3 = bf16[16,128,128]{2,1,0:T(8,128)(2,1)S(1)} async-done(((bf16[16,128,128]{2,1,0:T(8,128)(2,1)}), bf16[16,128,128]{2,1,0:T(8,128)(2,1)S(1)}, u32[]{:S(2)}, u32[]{:S(2)}) %all-to-all-start.3) | async-done | bytes 524320 | tf_op jit(solution)/shard_map/all_to_all | solution.py:128
  153.3 24.2 %all-gather.4.cloned.1.call-done = bf16[2048,2048]{1,0:T(8,128)(2,1)} async-done(((bf16[2048,128]{1,0:T(8,128)(2,1)}), bf16[2048,2048]{1,0:T(8,128)(2,1)}) %all-gather.4.cloned.1.call-update) | async-done | bytes 8388624 | tf_op jit(solution)/shard_map/all_gather | solution.py:114
  177.4 6.4 %fusion.28 = (f32[128]{0:T(128)S(1)}, bf16[128,2048]{1,0:T(8,128)(2,1)S(1)}) fusion(bf16[128,2048]{0,1:T(8,128)(2,1)S(1)} %bitcast.156, bf16[2048,2048]{1,0:T(8,128)(2,1)} %all-gather.4.cloned.1.call-done, bf16[128,2048]{1,0:T(8,128)(2,1)S(1)} %copy-done.1), kind=kOutput, calls=%fused_computation.32 | convolution fusion | flops 1075314560 | bytes 9961984 | tf_op jit(solution)/shard_map/tr,cr->tc/dot_general | solution.py:129
  184.6 19.6 %all_to_all.86 = bf16[16,16,2048]{2,1,0:T(8,128)(2,1)S(1)} all-to-all(bf16[16,16,2048]{2,1,0:T(8,128)(2,1)S(1)} %bitcast.153), channel_id=1, replica_groups=mesh['dh'=2,'dz'=16,'tensor'=16] {'tensor'}, dimensions={0} | all-to-all | bytes 2097152 | tf_op jit(solution)/shard_map/all_to_all | solution.py:150
  204.7 3.8 %convolution_convert_fusion = bf16[16,16,2048]{2,1,0:T(8,128)(2,1)} fusion(bf16[16,16,2048]{2,1,0:T(8,128)(2,1)S(1)} %all_to_all.86, bf16[1,256,2048]{1,2,0:T(8,128)(2,1)} %bitcast.159, bf16[1,2048,256]{2,1,0:T(8,128)(2,1)} %reshape_reshape.7, f32[16,16,256]{2,1,0:T(8,128)S(1)} %fusion.34), kind=kOutput, calls=%fused_computation.21 | convolution fusion | flops 537788416 | bytes 4456448 | tf_op jit(solution)/shard_map/smp,pd->smd/dot_general | solution.py:154
  208.5 4.7 %all-to-all-start.5 = ((bf16[16,16,2048]{2,1,0:T(8,128)(2,1)}), bf16[16,16,2048]{2,1,0:T(8,128)(2,1)S(1)}, u32[]{:S(2)}, u32[]{:S(2)}) async-start(bf16[16,16,2048]{2,1,0:T(8,128)(2,1)} %convolution_convert_fusion), calls=%async_computation.5 | async-start | bytes 2097152 | tf_op jit(solution)/shard_map/all_to_all | solution.py:157
  213.2 15.5 %all-to-all-done.5 = bf16[16,16,2048]{2,1,0:T(8,128)(2,1)S(1)} async-done(((bf16[16,16,2048]{2,1,0:T(8,128)(2,1)}), bf16[16,16,2048]{2,1,0:T(8,128)(2,1)S(1)}, u32[]{:S(2)}, u32[]{:S(2)}) %all-to-all-start.5) | async-done | bytes 1048608 | tf_op jit(solution)/shard_map/all_to_all | solution.py:157
  (85 shorter events, 32.9 us)
Async XLA Ops:
  7.2 10.5 %copy-start = (bf16[128,2048]{1,0:T(8,128)(2,1)S(1)}, bf16[128,2048]{1,0:T(8,128)(2,1)}, u32[]{:S(2)}) copy-start(bf16[128,2048]{1,0:T(8,128)(2,1)} %param.17) | copy-start | bytes 1572868
  7.2 36.4 %copy-start.9 = (s32[1,17]{1,0:T(1,128)S(1)}, s32[1,17]{1,0:T(1,128)}, u32[]{:S(2)}) copy-start(s32[1,17]{1,0:T(1,128)} %param.20) | copy-start | bytes 208
  7.2 36.5 %copy-start.3 = (bf16[128,2048]{1,0:T(8,128)(2,1)S(1)}, bf16[128,2048]{1,0:T(8,128)(2,1)}, u32[]{:S(2)}) copy-start(bf16[128,2048]{1,0:T(8,128)(2,1)} %param.16) | copy-start | bytes 1572868
  7.2 84.3 %all-gather.6.cloned.1.call-start = ((), (), s32[]{:S(2)}) async-start(), calls=%async_computation.7 | async-start | bytes 3899392 | tf_op jit(solution)/shard_map/all_gather | solution.py:108
  18.6 20.4 %all-to-all-start.1 = ((bf16[128,16,128]{2,0,1:T(8,128)(2,1)}), bf16[128,16,128]{2,0,1:T(8,128)(2,1)S(1)}, u32[]{:S(2)}, u32[]{:S(2)}) async-start(bf16[128,16,128]{2,0,1:T(8,128)(2,1)} %copy_bitcast_fusion.2), calls=%async_computation.1 | async-start | bytes 1048576 | tf_op jit(solution)/shard_map/all_to_all | solution.py:87
  38.9 56.8 %copy-start.4 = (bf16[128,16,128]{2,0,1:T(8,128)(2,1)}, bf16[128,16,128]{2,0,1:T(8,128)(2,1)S(1)}, u32[]{:S(2)}) copy-start(bf16[128,16,128]{2,0,1:T(8,128)(2,1)S(1)} %all-to-all-done.1) | copy-start | bytes 1572868
  38.9 14.4 %all-to-all-start.2 = ((bf16[128,16,128]{2,0,1:T(8,128)(2,1)}), bf16[128,16,128]{2,0,1:T(8,128)(2,1)S(1)}, u32[]{:S(2)}, u32[]{:S(2)}) async-start(bf16[128,16,128]{2,0,1:T(8,128)(2,1)} %copy_bitcast_fusion.1), calls=%async_computation.2 | async-start | bytes 1048576 | tf_op jit(solution)/shard_map/all_to_all | solution.py:88
  53.3 17.8 %all-to-all-start = ((bf16[128,16,128]{2,0,1:T(8,128)(2,1)}), bf16[128,16,128]{2,0,1:T(8,128)(2,1)S(1)}, u32[]{:S(2)}, u32[]{:S(2)}) async-start(bf16[128,16,128]{2,0,1:T(8,128)(2,1)} %copy_bitcast_fusion.3), calls=%async_computation | async-start | bytes 1048576 | tf_op jit(solution)/shard_map/all_to_all | solution.py:86
  57.9 119.5 %all-gather.4.cloned.1.call-start = ((), (), s32[]{:S(2)}) async-start(), calls=%async_computation.6 | async-start | bytes 8912896 | tf_op jit(solution)/shard_map/all_gather | solution.py:114
  71.1 24.6 %copy-start.6 = (bf16[128,16,128]{2,0,1:T(8,128)(2,1)}, bf16[128,16,128]{2,0,1:T(8,128)(2,1)S(1)}, u32[]{:S(2)}) copy-start(bf16[128,16,128]{2,0,1:T(8,128)(2,1)S(1)} %all-to-all-done) | copy-start | bytes 1572868
  104.7 4.0 %copy-start.5 = (bf16[128,16,128]{2,0,1:T(8,128)(2,1)S(1)}, bf16[128,16,128]{2,0,1:T(8,128)(2,1)}, u32[]{:S(2)}) copy-start(bf16[128,16,128]{2,0,1:T(8,128)(2,1)} %copy-done.4) | copy-start | bytes 1572868
  108.7 30.7 %copy-start.7 = (s32[128,8]{0,1:T(8,128)S(1)}, s32[128,8]{0,1:T(8,128)}, u32[]{:S(2)}) copy-start(s32[128,8]{0,1:T(8,128)} %param.26) | copy-start | bytes 12292
  108.7 68.8 %copy-start.1 = (bf16[128,2048]{1,0:T(8,128)(2,1)S(1)}, bf16[128,2048]{1,0:T(8,128)(2,1)}, u32[]{:S(2)}) copy-start(bf16[128,2048]{1,0:T(8,128)(2,1)} %param.15) | copy-start | bytes 1572868
  124.5 28.5 %all-to-all-start.3 = ((bf16[16,128,128]{2,1,0:T(8,128)(2,1)}), bf16[16,128,128]{2,1,0:T(8,128)(2,1)S(1)}, u32[]{:S(2)}, u32[]{:S(2)}) async-start(bf16[16,128,128]{2,1,0:T(8,128)(2,1)} %bitcast.39), calls=%async_computation.3 | async-start | bytes 1048576 | tf_op jit(solution)/shard_map/all_to_all | solution.py:128
  177.4 6.4 %copy-start.10 = (f32[2048]{0:T(1024)S(1)}, f32[2048]{0:T(1024)}, u32[]{:S(2)}) copy-start(f32[2048]{0:T(1024)} %param.22) | copy-start | bytes 24580
  183.8 0.8 copy-start.2
  204.2 8.9 %copy-start.8 = (f32[128,8]{0,1:T(8,128)S(1)}, f32[128,8]{0,1:T(8,128)}, u32[]{:S(2)}) copy-start(f32[128,8]{0,1:T(8,128)} %param.27) | copy-start | bytes 12292
  208.5 20.2 %all-to-all-start.5 = ((bf16[16,16,2048]{2,1,0:T(8,128)(2,1)}), bf16[16,16,2048]{2,1,0:T(8,128)(2,1)S(1)}, u32[]{:S(2)}, u32[]{:S(2)}) async-start(bf16[16,16,2048]{2,1,0:T(8,128)(2,1)} %convolution_convert_fusion), calls=%async_computation.5 | async-start | bytes 2097152 | tf_op jit(solution)/shard_map/all_to_all | solution.py:157
Sparse Core Ops, SparseCore 0:
  17.7 73.7 all-gather.5
  93.6 83.7 all-gather.3

commit v5 on v4

--- a/solution.py
+++ b/solution.py
@@ -106,8 +106,10 @@
     pieces = [wo_shard.T, gate_shard[0], up_shard[0], down_shard[0]]
     packed = jnp.concatenate([p.reshape(-1) for p in pieces]).astype(jnp.bfloat16).reshape(-1, 128)
     gathered = lax.all_gather(lax.all_gather(packed, "dh"), "dz")
-    gathered, q_heads, k_heads, v_heads, key_pages, value_pages = lax.optimization_barrier(
-        (gathered, q_heads, k_heads, v_heads, key_pages, value_pages)
+    attended = attend_group(q_heads, k_heads, v_heads, segment, heads_here)
+    token_rows = lax.all_to_all(attended, "tensor", split_axis=0, concat_axis=1, tiled=True)
+    gathered, token_rows, key_pages, value_pages = lax.optimization_barrier(
+        (gathered, token_rows, key_pages, value_pages)
     )
     wo_piece_rows = pieces[0].size // 128
     wo_cols = jnp.swapaxes(gathered[:, :, :wo_piece_rows], 0, 1).reshape(-1, pieces[0].shape[1])
@@ -118,22 +120,10 @@
     for p in pieces[1:]:
         weights_full.append(experts[:, at : at + p.size].reshape((-1,) + p.shape))
         at += p.size
-    gate_full = weights_full[0].reshape(1, -1, gate_shard.shape[2])
-    up_full = weights_full[1].reshape(1, -1, up_shard.shape[2])
-    down_full = weights_full[2].transpose(1, 0, 2).reshape(1, down_shard.shape[1], -1)
-    attended = attend_group(q_heads, k_heads, v_heads, segment, heads_here)
-    attended, gate_full, up_full, down_full = lax.optimization_barrier(
-        (attended, gate_full, up_full, down_full)
-    )
-    token_rows = lax.all_to_all(attended, "tensor", split_axis=0, concat_axis=1, tiled=True)
-    projected = jnp.einsum("tr,cr->tc", token_rows, wo_full, preferred_element_type=jnp.float32)
-    hidden_mid = (residual.astype(jnp.float32) + projected).astype(jnp.bfloat16)
-    mid_float = hidden_mid.astype(jnp.float32)
-    normed = (
-        mid_float
-        * lax.rsqrt(jnp.mean(mid_float * mid_float, axis=1, keepdims=True) + 1e-06)
-        * norm_gain
-    ).astype(jnp.bfloat16)
+    gate_full = weights_full[0].reshape(-1, gate_shard.shape[2])
+    up_full = weights_full[1].reshape(-1, up_shard.shape[2])
+    down_full = weights_full[2].transpose(1, 0, 2).reshape(down_shard.shape[1], -1)
+
     flight = tensor_count // SPLIT
     flight_ids = jnp.arange(flight, dtype=jnp.int32)
     named_here = routes[:, :, None] == flight_ids[None, None, :]
@@ -143,18 +133,42 @@
     picked = (ranked[:, :, None] == jnp.arange(MOST, dtype=jnp.int32)[None, None, :]) & routed[
         :, :, None
     ]
-    outgoing = jnp.einsum(
-        "tem,td->emd", picked.astype(jnp.bfloat16), normed, preferred_element_type=jnp.float32
+    selector = picked.astype(jnp.bfloat16)
+    outgoing = jnp.concatenate(
+        [
+            jnp.einsum("tem,td->emd", selector, token_rows, preferred_element_type=jnp.float32),
+            jnp.einsum("tem,td->emd", selector, residual, preferred_element_type=jnp.float32),
+        ],
+        axis=2,
     ).astype(jnp.bfloat16)
     outgoing = jnp.repeat(outgoing, SPLIT, axis=0)
+    outgoing, gate_full, up_full, down_full = lax.optimization_barrier(
+        (outgoing, gate_full, up_full, down_full)
+    )
     arrived = lax.all_to_all(outgoing, "tensor", split_axis=0, concat_axis=0, tiled=True)
-    gate_val = jnp.einsum("smd,dp->smp", arrived, gate_full[0], preferred_element_type=jnp.float32)
-    up_val = jnp.einsum("smd,dp->smp", arrived, up_full[0], preferred_element_type=jnp.float32)
+
+    def project_norm(rows_att, rows_res):
+        projected = jnp.einsum(
+            "...r,cr->...c", rows_att, wo_full, preferred_element_type=jnp.float32
+        )
+        mid = (rows_res.astype(jnp.float32) + projected).astype(jnp.bfloat16)
+        mid_float = mid.astype(jnp.float32)
+        normed = (
+            mid_float
+            * lax.rsqrt(jnp.mean(mid_float * mid_float, axis=-1, keepdims=True) + 1e-06)
+            * norm_gain
+        ).astype(jnp.bfloat16)
+        return mid, normed
+
+    _, arrived_normed = project_norm(arrived[:, :, :D], arrived[:, :, D:])
+    gate_val = jnp.einsum("smd,dp->smp", arrived_normed, gate_full, preferred_element_type=jnp.float32)
+    up_val = jnp.einsum("smd,dp->smp", arrived_normed, up_full, preferred_element_type=jnp.float32)
     inner_act = (jax.nn.silu(gate_val) * up_val).astype(jnp.bfloat16)
     result = jnp.einsum(
-        "smp,pd->smd", inner_act, down_full[0], preferred_element_type=jnp.float32
+        "smp,pd->smd", inner_act, down_full, preferred_element_type=jnp.float32
     ).astype(jnp.bfloat16)
     returned = lax.all_to_all(result, "tensor", split_axis=0, concat_axis=0, tiled=True)
+    hidden_mid, _ = project_norm(token_rows, residual)
     summed = jnp.sum(returned.reshape(flight, SPLIT, MOST, D).astype(jnp.float32), axis=1)
     mixing = picked.astype(jnp.float32) * weight_sum[:, :, None]
     expert_sum = jnp.einsum("tem,emd->td", mixing, summed, precision=lax.Precision.HIGHEST).astype(

time: 239 us -> 241 us (level)
  blocking collectives: 26.3 us -> 58.8 us
  waiting for transfers between devices: 88 us -> 62.9 us
  starting transfers between devices: 39.4 us -> 29.3 us
  matrix products: 25.7 us -> 29.6 us
    all_to_all x1, blocking collectives: 19.6 us -> 51.4 us  [body(): lax.all_to_all(outgoing, 'tensor', split_axis=0, concat_axis=0, tiled=True)]
    all_to_all x1, waiting for transfers between devices: 13.3 us -> 0.01 us  [body(): lax.all_to_all(attended, 'tensor', split_axis=0, concat_axis=1, tiled=True)]
    all_gather x1, waiting for transfers between devices: 20.4 us -> 7.38 us  [body(): gathered = lax.all_gather(lax.all_gather(packed, 'dh'), 'dz')]
    all_to_all x1, starting transfers between devices: 14.8 us -> 4.72 us  [body(): lax.all_to_all(attended, 'tensor', split_axis=0, concat_axis=1, tiled=True)]
    all_to_all x1, waiting for transfers between devices: 0.01 us -> 8.81 us  [body(): lax.all_to_all(queries, 'tensor', split_axis=1, concat_axis=0, tiled=True)]
    dot_general x4 -> x6, matrix products: 10.9 us -> 18.4 us  [the longest x2 13 us: project_norm(): jnp.einsum('...r,cr->...c', rows_att, wo_full, preferred_element_type=jnp...]
    all_to_all x1, waiting for transfers between devices: 15.5 us -> 8.36 us  [body(): lax.all_to_all(result, 'tensor', split_axis=0, concat_axis=0, tiled=True)]
    all_to_all x1, waiting for transfers between devices: 5.9 us -> 0.01 us  [body(): lax.all_to_all(new_keys, 'tensor', split_axis=1, concat_axis=0, tiled=True)]
  transfers between devices with their start and end apart: 7 -> 7, of which waited for: 6 -> 5; matrix products, arithmetic and copies ran while one was open for 21% -> 24% of each run, Pallas kernels for 0% -> 0%
where the time goes in v5:
time: 241 us; the launch traced here: 240 us
  waiting for transfers between devices  62.9 us (26%)
  blocking collectives  58.8 us (24%)
  local copies, waits for them, and re-layouts  37.5 us (16%)
  matrix products  29.6 us (12%)
  starting transfers between devices  29.3 us (12%)
  between operations  14.3 us (6%)
  other arithmetic  7.31 us (3%)
    all_to_all x1, blocking collectives, body(): lax.all_to_all(outgoing, 'tensor', split_axis=0, concat_axis=0, tiled=True)  51.4 us
    all_gather x1, waiting for transfers between devices, body(): wo_full = lax.all_gather(wo_cols, 'tensor', axis=1, tiled=True)  30 us
    dot_general x2, matrix products, project_norm(): jnp.einsum('...r,cr->...c', rows_att, wo_full, preferred_element_type=jnp...  13 us
    all_to_all x1, starting transfers between devices, body(): lax.all_to_all(new_keys, 'tensor', split_axis=1, concat_axis=0, tiled=True)  10.2 us
    all_to_all x1, waiting for transfers between devices, body(): lax.all_to_all(queries, 'tensor', split_axis=1, concat_axis=0, tiled=True)  8.81 us
    all_to_all x1, waiting for transfers between devices, body(): lax.all_to_all(result, 'tensor', split_axis=0, concat_axis=0, tiled=True)  8.36 us
    all_to_all x1, waiting for transfers between devices, body(): lax.all_to_all(new_values, 'tensor', split_axis=1, concat_axis=0, tiled=T...  8.32 us
    all_gather x1, blocking collectives, body(): gathered = lax.all_gather(lax.all_gather(packed, 'dh'), 'dz')  7.42 us
  transfers between devices with their start and end apart: 7, of which 5 were waited for; matrix products, arithmetic and copies ran while one was open for 24% of the time, Pallas kernels for 0%

profile of v5, /device:TPU:1, one launch (start us, length us, event | category | flops | bytes accessed | tf_op | source)
XLA Modules:
  0.0 239.8 jit_solution(5962493539919212022)
XLA Ops:
  7.2 2.1 copy.93
  9.3 10.2 %all-to-all-start.1 = ((bf16[128,16,128]{0,2,1:T(8,128)(2,1)}), bf16[128,16,128]{0,2,1:T(8,128)(2,1)S(1)}, u32[]{:S(2)}, u32[]{:S(2)}) async-start(bf16[128,16,128]{0,2,1:T(8,128)(2,1)} %bitcast.18), calls=%async_computation.1 | async-start | bytes 1048576 | tf_op jit(solution)/shard_map/all_to_all | solution.py:87
  23.2 7.4 %all_gather.12 = bf16[2,448,128]{2,1,0:T(8,128)(2,1)} all-gather(bf16[1,448,128]{2,1,0:T(8,128)(2,1)S(1)} %maximum_bitcast_fusion), channel_id=1, replica_groups=mesh['dh'=2,'dz'=16,'tensor'=16] {'dh'}, dimensions={0}, use_global_device_ids=true | all-gather | bytes 344064 | tf_op jit(solution)/shard_map/all_gather | solution.py:108
  31.6 5.8 %all-to-all-start.2 = ((bf16[128,16,128]{0,2,1:T(8,128)(2,1)}), bf16[128,16,128]{0,2,1:T(8,128)(2,1)S(1)}, u32[]{:S(2)}, u32[]{:S(2)}) async-start(bf16[128,16,128]{0,2,1:T(8,128)(2,1)} %bitcast.21), calls=%async_computation.2 | async-start | bytes 1048576 | tf_op jit(solution)/shard_map/all_to_all | solution.py:88
  38.8 8.3 %all-to-all-done.2 = bf16[128,16,128]{0,2,1:T(8,128)(2,1)S(1)} async-done(((bf16[128,16,128]{0,2,1:T(8,128)(2,1)}), bf16[128,16,128]{0,2,1:T(8,128)(2,1)S(1)}, u32[]{:S(2)}, u32[]{:S(2)}) %all-to-all-start.2) | async-done | bytes 524320 | tf_op jit(solution)/shard_map/all_to_all | solution.py:88
  47.2 4.6 %all-to-all-start = ((bf16[128,16,128]{0,2,1:T(8,128)(2,1)}), bf16[128,16,128]{0,2,1:T(8,128)(2,1)S(1)}, u32[]{:S(2)}, u32[]{:S(2)}) async-start(bf16[128,16,128]{0,2,1:T(8,128)(2,1)} %bitcast.14), calls=%async_computation | async-start | bytes 1048576 | tf_op jit(solution)/shard_map/all_to_all | solution.py:86
  52.7 8.8 %all-to-all-done = bf16[128,16,128]{0,2,1:T(8,128)(2,1)S(1)} async-done(((bf16[128,16,128]{0,2,1:T(8,128)(2,1)}), bf16[128,16,128]{0,2,1:T(8,128)(2,1)S(1)}, u32[]{:S(2)}, u32[]{:S(2)}) %all-to-all-start) | async-done | bytes 524320 | tf_op jit(solution)/shard_map/all_to_all | solution.py:86
  61.8 12.3 %while.10 = (s32[]{:T(128)}, bf16[4,512,128]{2,1,0:T(8,128)(2,1)}, s32[4,512]{1,0:T(4,128)S(1)}, s32[2048]{0:T(1024)S(1)}, bf16[4,512,1,128]{3,1,2,0:T(8,128)(2,...) while((s32[]{:T(128)}, bf16[4,512,128]{2,1,0:T(8,128)(2,1)}, ...), condition=%wide.region_5.6_spmd, body=%wide.region_2.0_spmd.sunk | while | flops 545389568 | bytes 13918813 | solution.py:65
  74.0 4.7 %all-to-all-start.3 = ((bf16[16,128,128]{2,1,0:T(8,128)(2,1)}), bf16[16,128,128]{2,1,0:T(8,128)(2,1)S(1)}, u32[]{:S(2)}, u32[]{:S(2)}) async-start(bf16[16,128,128]{2,1,0:T(8,128)(2,1)} %bitcast.24), calls=%async_computation.3 | async-start | bytes 1048576 | tf_op jit(solution)/shard_map/all_to_all | solution.py:110
  78.9 6.5 %scatter_custom_fusion = bf16[2176,128]{1,0:T(8,128)(2,1)} fusion(s32[2048]{0:T(1024)S(1)} %bitcast.164, bf16[2048,128]{1,0:T(8,128)(2,1)S(1)} %bitcast.157, bf16[]{:T(256)} %constant.81.clone.1), kind=kCustom, calls=%fused_computation.52 | custom fusion | bytes 557058 | tf_op jit(solution)/shard_map/scatter | solution.py:97
  85.4 6.5 %scatter_custom_fusion.1 = bf16[2176,128]{1,0:T(8,128)(2,1)} fusion(s32[2048]{0:T(1024)S(1)} %bitcast.165, bf16[2048,128]{1,0:T(8,128)(2,1)S(1)} %bitcast.142, bf16[]{:T(256)} %constant.81.clone.1), kind=kCustom, calls=%fused_computation.50 | custom fusion | bytes 557058 | tf_op jit(solution)/shard_map/scatter | solution.py:103
  92.0 7.4 %all-gather.6.cloned.1.call-done = bf16[32,448,128]{2,1,0:T(8,128)(2,1)} async-done(((bf16[2,448,128]{2,1,0:T(8,128)(2,1)}), bf16[32,448,128]{2,1,0:T(8,128)(2,1)}) %all-gather.6.cloned.1.call-update) | async-done | bytes 3670032 | tf_op jit(solution)/shard_map/all_gather | solution.py:108
  102.0 2.2 slice_bitcast_fusion
  104.6 2.0 copy.115
  108.4 3.0 %reshape.265 = bf16[32,256,64]{2,1,0:T(8,128)(2,1)S(1)} reshape(bf16[32,16384]{1,0:T(8,128)(2,1)} %get-tuple-element.111) | data formatting | bytes 2097152 | tf_op jit(solution)/shard_map/reshape | solution.py:121
  113.2 2.3 reshape_reshape.6
  115.5 2.3 reshape_reshape.7
  118.4 51.4 %all_to_all.83 = bf16[16,16,4096]{2,1,0:T(8,128)(2,1)S(1)} all-to-all(bf16[16,16,4096]{2,1,0:T(8,128)(2,1)S(1)} %bitcast.146), channel_id=1, replica_groups=mesh['dh'=2,'dz'=16,'tensor'=16] {'tensor'}, dimensions={0} | all-to-all | bytes 4194304 | tf_op jit(solution)/shard_map/all_to_all | solution.py:148
  169.8 30.0 %all-gather.4.cloned.1.call-done = bf16[2048,2048]{1,0:T(8,128)(2,1)} async-done(((bf16[2048,128]{1,0:T(8,128)(2,1)}), bf16[2048,2048]{1,0:T(8,128)(2,1)}) %all-gather.4.cloned.1.call-update) | async-done | bytes 8388624 | tf_op jit(solution)/shard_map/all_gather | solution.py:116
  199.8 6.0 %fusion.35 = (f32[16,16]{1,0:T(8,128)S(1)}, bf16[16,16,2048]{2,1,0:T(8,128)(2,1)S(1)}) fusion(bf16[2048,2048]{1,0:T(8,128)(2,1)} %all-gather.4.cloned.1.call-done, bf16[16,16,4096]{2,1,0:T(8,128)(2,1)S(1)} %all_to_all.83), kind=kOutput, calls=%fused_computation.34 | convolution fusion | flops 2150629120 | bytes 11535360 | tf_op jit(solution)/shard_map/...r,cr->...c/dot_general | solution.py:151
  207.9 3.7 %convolution_convert_fusion = bf16[16,16,2048]{2,1,0:T(8,128)(2,1)} fusion(bf16[256,2048]{0,1:T(8,128)(2,1)S(1)} %bitcast.153, bf16[2048,256]{1,0:T(8,128)(2,1)S(1)} %copy-done.3, bf16[16,16,2048]{2,1,0:T(8,128)(2,1)} %copy-done.11, f32[2048]{0:T(1024)S(1)} %copy-done.10, f32[16,16]{1,0:T(8,128)S(1)} %add_rsqrt_fusion, f32[16,16,256]{2,1,0:T(8,128)} %fusion.43), kind=kOutput, calls=%fused_computation.27 | convolution fusion | flops 539885568 | bytes 4465664 | tf_op jit(solution)/shard_map/smp,pd->smd/dot_general | solution.py:167
  211.6 3.9 %all-to-all-start.5 = ((bf16[16,16,2048]{2,1,0:T(8,128)(2,1)}), bf16[16,16,2048]{2,1,0:T(8,128)(2,1)S(1)}, u32[]{:S(2)}, u32[]{:S(2)}) async-start(bf16[16,16,2048]{2,1,0:T(8,128)(2,1)} %convolution_convert_fusion), calls=%async_computation.5 | async-start | bytes 2097152 | tf_op jit(solution)/shard_map/all_to_all | solution.py:170
  215.6 7.1 %fusion.33 = bf16[128,2048]{1,0:T(8,128)(2,1)} fusion(bf16[128,2048]{1,0:T(8,128)(2,1)S(1)} %copy_bitcast_fusion.1, bf16[2048,2048]{1,0:T(8,128)(2,1)} %all-gather.4.cloned.1.call-done, bf16[128,2048]{1,0:T(8,128)(2,1)S(1)} %copy-done), kind=kOutput, calls=%fused_computation.30 | convolution fusion | flops 1074528256 | bytes 9961472 | tf_op jit(solution)/shard_map/...r,cr->...c/dot_general | solution.py:151
  222.6 8.4 %all-to-all-done.5 = bf16[16,16,2048]{2,1,0:T(8,128)(2,1)S(1)} async-done(((bf16[16,16,2048]{2,1,0:T(8,128)(2,1)}), bf16[16,16,2048]{2,1,0:T(8,128)(2,1)S(1)}, u32[]{:S(2)}, u32[]{:S(2)}) %all-to-all-start.5) | async-done | bytes 1048608 | tf_op jit(solution)/shard_map/all_to_all | solution.py:170
  (93 shorter events, 30.7 us)
Async XLA Ops:
  7.2 23.5 %copy-start.4 = (bf16[128,2048]{1,0:T(8,128)(2,1)S(1)}, bf16[128,2048]{1,0:T(8,128)(2,1)}, u32[]{:S(2)}) copy-start(bf16[128,2048]{1,0:T(8,128)(2,1)} %param.18) | copy-start | bytes 1572868
  7.2 30.3 %copy-start.9 = (s32[1,2]{1,0:T(1,128)S(1)}, s32[1,2]{1,0:T(1,128)}, u32[]{:S(2)}) copy-start(s32[1,2]{1,0:T(1,128)} %param.19) | copy-start | bytes 28
  7.2 30.6 %copy-start.5 = (bf16[128,2048]{1,0:T(8,128)(2,1)S(1)}, bf16[128,2048]{1,0:T(8,128)(2,1)}, u32[]{:S(2)}) copy-start(bf16[128,2048]{1,0:T(8,128)(2,1)} %param.16) | copy-start | bytes 1572868
  9.3 22.3 %all-to-all-start.1 = ((bf16[128,16,128]{0,2,1:T(8,128)(2,1)}), bf16[128,16,128]{0,2,1:T(8,128)(2,1)S(1)}, u32[]{:S(2)}, u32[]{:S(2)}) async-start(bf16[128,16,128]{0,2,1:T(8,128)(2,1)} %bitcast.18), calls=%async_computation.1 | async-start | bytes 1048576 | tf_op jit(solution)/shard_map/all_to_all | solution.py:87
  19.5 32.5 %copy-start.8 = (s32[1,17]{1,0:T(1,128)S(1)}, s32[1,17]{1,0:T(1,128)}, u32[]{:S(2)}) copy-start(s32[1,17]{1,0:T(1,128)} %param.20) | copy-start | bytes 208
  19.5 79.9 %all-gather.6.cloned.1.call-start = ((), (), s32[]{:S(2)}) async-start(), calls=%async_computation.7 | async-start | bytes 3899392 | tf_op jit(solution)/shard_map/all_gather | solution.py:108
  31.6 15.5 %all-to-all-start.2 = ((bf16[128,16,128]{0,2,1:T(8,128)(2,1)}), bf16[128,16,128]{0,2,1:T(8,128)(2,1)S(1)}, u32[]{:S(2)}, u32[]{:S(2)}) async-start(bf16[128,16,128]{0,2,1:T(8,128)(2,1)} %bitcast.21), calls=%async_computation.2 | async-start | bytes 1048576 | tf_op jit(solution)/shard_map/all_to_all | solution.py:88
  47.2 14.3 %all-to-all-start = ((bf16[128,16,128]{0,2,1:T(8,128)(2,1)}), bf16[128,16,128]{0,2,1:T(8,128)(2,1)S(1)}, u32[]{:S(2)}, u32[]{:S(2)}) async-start(bf16[128,16,128]{0,2,1:T(8,128)(2,1)} %bitcast.14), calls=%async_computation | async-start | bytes 1048576 | tf_op jit(solution)/shard_map/all_to_all | solution.py:86
  74.0 27.3 %copy-start.6 = (s32[128,8]{0,1:T(8,128)S(1)}, s32[128,8]{0,1:T(8,128)}, u32[]{:S(2)}) copy-start(s32[128,8]{0,1:T(8,128)} %param.26) | copy-start | bytes 12292
  74.0 27.7 %copy-start = (bf16[128,2048]{1,0:T(8,128)(2,1)S(1)}, bf16[128,2048]{1,0:T(8,128)(2,1)}, u32[]{:S(2)}) copy-start(bf16[128,2048]{1,0:T(8,128)(2,1)} %param.15) | copy-start | bytes 1572868
  74.0 17.9 %all-to-all-start.3 = ((bf16[16,128,128]{2,1,0:T(8,128)(2,1)}), bf16[16,128,128]{2,1,0:T(8,128)(2,1)S(1)}, u32[]{:S(2)}, u32[]{:S(2)}) async-start(bf16[16,128,128]{2,1,0:T(8,128)(2,1)} %bitcast.24), calls=%async_computation.3 | async-start | bytes 1048576 | tf_op jit(solution)/shard_map/all_to_all | solution.py:110
  78.8 121.0 %all-gather.4.cloned.1.call-start = ((), (), s32[]{:S(2)}) async-start(), calls=%async_computation.6 | async-start | bytes 8912896 | tf_op jit(solution)/shard_map/all_gather | solution.py:116
  169.8 36.9 %copy-start.10 = (f32[2048]{0:T(1024)S(1)}, f32[2048]{0:T(1024)}, u32[]{:S(2)}) copy-start(f32[2048]{0:T(1024)} %param.22) | copy-start | bytes 24580
  199.8 7.0 %copy-start.2 = (bf16[2048,256]{1,0:T(8,128)(2,1)S(1)}, bf16[2048,256]{1,0:T(8,128)(2,1)}, u32[]{:S(2)}) copy-start(bf16[2048,256]{1,0:T(8,128)(2,1)} %reshape_reshape.6) | copy-start | bytes 3145732
  205.8 1.0 copy-start.11
  205.8 2.2 copy-start.1
  205.8 2.2 copy-start.3
  207.9 7.6 %copy-start.7 = (f32[128,8]{0,1:T(8,128)S(1)}, f32[128,8]{0,1:T(8,128)}, u32[]{:S(2)}) copy-start(f32[128,8]{0,1:T(8,128)} %param.27) | copy-start | bytes 12292
  211.6 19.4 %all-to-all-start.5 = ((bf16[16,16,2048]{2,1,0:T(8,128)(2,1)}), bf16[16,16,2048]{2,1,0:T(8,128)(2,1)S(1)}, u32[]{:S(2)}, u32[]{:S(2)}) async-start(bf16[16,16,2048]{2,1,0:T(8,128)(2,1)} %convolution_convert_fusion), calls=%async_computation.5 | async-start | bytes 2097152 | tf_op jit(solution)/shard_map/all_to_all | solution.py:170
Sparse Core Ops, SparseCore 0:
  30.8 68.6 all-gather.5
  102.0 97.6 all-gather.3

commit v6 on v5

--- a/solution.py
+++ b/solution.py
@@ -82,6 +82,12 @@
 ):
     tensor_count = lax.axis_size("tensor")
     heads_here = HEADS // tensor_count
+    pieces = [wo_shard.T, gate_shard[0], up_shard[0], down_shard[0]]
+    packed = jnp.concatenate([p.reshape(-1) for p in pieces]).astype(jnp.bfloat16).reshape(-1, 128)
+    pairs = lax.all_gather(packed, "dh")
+    pairs, queries, new_keys, new_values = lax.optimization_barrier(
+        (pairs, queries, new_keys, new_values)
+    )
     q_heads, k_heads, v_heads = (
         lax.all_to_all(queries, "tensor", split_axis=1, concat_axis=0, tiled=True),
         lax.all_to_all(new_keys, "tensor", split_axis=1, concat_axis=0, tiled=True),
@@ -103,27 +109,9 @@
         .set(v_heads)
         .reshape(pool_size, PAGE, head_width)
     )
-    pieces = [wo_shard.T, gate_shard[0], up_shard[0], down_shard[0]]
-    packed = jnp.concatenate([p.reshape(-1) for p in pieces]).astype(jnp.bfloat16).reshape(-1, 128)
-    gathered = lax.all_gather(lax.all_gather(packed, "dh"), "dz")
+    gathered = lax.all_gather(pairs, "dz")
     attended = attend_group(q_heads, k_heads, v_heads, segment, heads_here)
     token_rows = lax.all_to_all(attended, "tensor", split_axis=0, concat_axis=1, tiled=True)
-    gathered, token_rows, key_pages, value_pages = lax.optimization_barrier(
-        (gathered, token_rows, key_pages, value_pages)
-    )
-    wo_piece_rows = pieces[0].size // 128
-    wo_cols = jnp.swapaxes(gathered[:, :, :wo_piece_rows], 0, 1).reshape(-1, pieces[0].shape[1])
-    wo_full = lax.all_gather(wo_cols, "tensor", axis=1, tiled=True)
-    experts = jnp.swapaxes(gathered[:, :, wo_piece_rows:], 0, 1)
-    experts = experts.reshape(experts.shape[0] * experts.shape[1], -1)
-    weights_full, at = [], 0
-    for p in pieces[1:]:
-        weights_full.append(experts[:, at : at + p.size].reshape((-1,) + p.shape))
-        at += p.size
-    gate_full = weights_full[0].reshape(-1, gate_shard.shape[2])
-    up_full = weights_full[1].reshape(-1, up_shard.shape[2])
-    down_full = weights_full[2].transpose(1, 0, 2).reshape(down_shard.shape[1], -1)
-
     flight = tensor_count // SPLIT
     flight_ids = jnp.arange(flight, dtype=jnp.int32)
     named_here = routes[:, :, None] == flight_ids[None, None, :]
@@ -142,10 +130,24 @@
         axis=2,
     ).astype(jnp.bfloat16)
     outgoing = jnp.repeat(outgoing, SPLIT, axis=0)
-    outgoing, gate_full, up_full, down_full = lax.optimization_barrier(
-        (outgoing, gate_full, up_full, down_full)
-    )
     arrived = lax.all_to_all(outgoing, "tensor", split_axis=0, concat_axis=0, tiled=True)
+    gathered, arrived, token_rows = lax.optimization_barrier((gathered, arrived, token_rows))
+    wo_piece_rows = pieces[0].size // 128
+    wo_cols = jnp.swapaxes(gathered[:, :, :wo_piece_rows], 0, 1).reshape(-1, pieces[0].shape[1])
+    wo_full = lax.all_gather(wo_cols, "tensor", axis=1, tiled=True)
+    experts = jnp.swapaxes(gathered[:, :, wo_piece_rows:], 0, 1)
+    experts = experts.reshape(experts.shape[0] * experts.shape[1], -1)
+    weights_full, at = [], 0
+    for p in pieces[1:]:
+        weights_full.append(experts[:, at : at + p.size].reshape((-1,) + p.shape))
+        at += p.size
+    gate_full = weights_full[0].reshape(-1, gate_shard.shape[2])
+    up_full = weights_full[1].reshape(-1, up_shard.shape[2])
+    down_full = weights_full[2].transpose(1, 0, 2).reshape(down_shard.shape[1], -1)
+
+    arrived, key_pages, value_pages, gate_full, up_full, down_full = lax.optimization_barrier(
+        (arrived, key_pages, value_pages, gate_full, up_full, down_full)
+    )
 
     def project_norm(rows_att, rows_res):
         projected = jnp.einsum(

time: 241 us -> 251 us (1.041)
  waiting for transfers between devices: 62.9 us -> 121 us
  blocking collectives: 58.8 us -> 6.67 us
  starting transfers between devices: 29.3 us -> 33.4 us
  matrix products: 29.6 us -> 26.4 us
    all_to_all x1 -> x0, blocking collectives: 51.4 us -> none  [body(): lax.all_to_all(outgoing, 'tensor', split_axis=0, concat_axis=0, tiled=True)]
    all_to_all x0 -> x1, waiting for transfers between devices: none -> 26 us  [body(): lax.all_to_all(outgoing, 'tensor', split_axis=0, concat_axis=0, tiled=True)]
    all_gather x1, waiting for transfers between devices: 30 us -> 49.4 us  [body(): wo_full = lax.all_gather(wo_cols, 'tensor', axis=1, tiled=True)]
    all_to_all x1, waiting for transfers between devices: 0.01 us -> 9.11 us  [body(): lax.all_to_all(attended, 'tensor', split_axis=0, concat_axis=1, tiled=True)]
    all_to_all x1, waiting for transfers between devices: 0.01 us -> 8.75 us  [body(): lax.all_to_all(new_keys, 'tensor', split_axis=1, concat_axis=0, tiled=True)]
    all_gather x1, waiting for transfers between devices: 7.38 us -> 2.27 us  [body(): gathered = lax.all_gather(pairs, 'dz')]
    all_to_all x0 -> x1, starting transfers between devices: none -> 4.89 us  [body(): lax.all_to_all(outgoing, 'tensor', split_axis=0, concat_axis=0, tiled=True)]
    optimization_barrier x0 -> x3, local copies, waits for them, and re-layouts: none -> 4.05 us  [body(): lax.optimization_barrier((pairs, queries, new_keys, new_values))]
  transfers between devices with their start and end apart: 7 -> 8, of which waited for: 5 -> 8; matrix products, arithmetic and copies ran while one was open for 24% -> 21% of each run, Pallas kernels for 0% -> 0%
where the time goes in v6:
time: 251 us; the launch traced here: 250 us
  waiting for transfers between devices  121 us (48%)
  local copies, waits for them, and re-layouts  39.8 us (16%)
  starting transfers between devices  33.4 us (13%)
  matrix products  26.4 us (11%)
  between operations  14.4 us (6%)
  other arithmetic  7.42 us (3%)
  blocking collectives  6.67 us (3%)
    all_gather x1, waiting for transfers between devices, body(): wo_full = lax.all_gather(wo_cols, 'tensor', axis=1, tiled=True)  49.4 us
    all_to_all x1, waiting for transfers between devices, body(): lax.all_to_all(outgoing, 'tensor', split_axis=0, concat_axis=0, tiled=True)  26 us
    dot_general x2, matrix products, project_norm(): jnp.einsum('...r,cr->...c', rows_att, wo_full, preferred_element_type=jnp...  13 us
    all_to_all x1, starting transfers between devices, body(): lax.all_to_all(new_keys, 'tensor', split_axis=1, concat_axis=0, tiled=True)  10.6 us
    all_to_all x1, waiting for transfers between devices, body(): lax.all_to_all(attended, 'tensor', split_axis=0, concat_axis=1, tiled=True)  9.11 us
    all_to_all x1, waiting for transfers between devices, body(): lax.all_to_all(new_keys, 'tensor', split_axis=1, concat_axis=0, tiled=True)  8.75 us
    all_to_all x1, waiting for transfers between devices, body(): lax.all_to_all(new_values, 'tensor', split_axis=1, concat_axis=0, tiled=T...  8.75 us
    all_to_all x1, waiting for transfers between devices, body(): lax.all_to_all(result, 'tensor', split_axis=0, concat_axis=0, tiled=True)  8.34 us
  transfers between devices with their start and end apart: 8, of which 8 were waited for; matrix products, arithmetic and copies ran while one was open for 21% of the time, Pallas kernels for 0%

profile of v6, /device:TPU:1, one launch (start us, length us, event | category | flops | bytes accessed | tf_op | source)
XLA Modules:
  0.0 249.5 jit_solution(8391363832846303963)
XLA Ops:
  10.9 6.7 %all_gather.12 = bf16[2,448,128]{2,1,0:T(8,128)(2,1)} all-gather(bf16[1,448,128]{2,1,0:T(8,128)(2,1)S(1)} %maximum_bitcast_fusion), channel_id=1, replica_groups=mesh['dh'=2,'dz'=16,'tensor'=16] {'dh'}, dimensions={0}, use_global_device_ids=true | all-gather | bytes 344064 | tf_op jit(solution)/shard_map/all_gather | solution.py:87
  19.6 10.6 %all-to-all-start.1 = ((bf16[128,16,128]{0,2,1:T(8,128)(2,1)}), bf16[128,16,128]{0,2,1:T(8,128)(2,1)S(1)}, u32[]{:S(2)}, u32[]{:S(2)}) async-start(bf16[128,16,128]{0,2,1:T(8,128)(2,1)} %bitcast.18), calls=%async_computation.1 | async-start | bytes 1048576 | tf_op jit(solution)/shard_map/all_to_all | solution.py:93
  31.2 8.7 %all-to-all-done.1 = bf16[128,16,128]{0,2,1:T(8,128)(2,1)S(1)} async-done(((bf16[128,16,128]{0,2,1:T(8,128)(2,1)}), bf16[128,16,128]{0,2,1:T(8,128)(2,1)S(1)}, u32[]{:S(2)}, u32[]{:S(2)}) %all-to-all-start.1) | async-done | bytes 524320 | tf_op jit(solution)/shard_map/all_to_all | solution.py:93
  40.0 4.6 %all-to-all-start.2 = ((bf16[128,16,128]{0,2,1:T(8,128)(2,1)}), bf16[128,16,128]{0,2,1:T(8,128)(2,1)S(1)}, u32[]{:S(2)}, u32[]{:S(2)}) async-start(bf16[128,16,128]{0,2,1:T(8,128)(2,1)} %bitcast.21), calls=%async_computation.2 | async-start | bytes 1048576 | tf_op jit(solution)/shard_map/all_to_all | solution.py:94
  45.6 8.7 %all-to-all-done.2 = bf16[128,16,128]{0,2,1:T(8,128)(2,1)S(1)} async-done(((bf16[128,16,128]{0,2,1:T(8,128)(2,1)}), bf16[128,16,128]{0,2,1:T(8,128)(2,1)S(1)}, u32[]{:S(2)}, u32[]{:S(2)}) %all-to-all-start.2) | async-done | bytes 524320 | tf_op jit(solution)/shard_map/all_to_all | solution.py:94
  54.3 4.6 %all-to-all-start = ((bf16[128,16,128]{0,2,1:T(8,128)(2,1)}), bf16[128,16,128]{0,2,1:T(8,128)(2,1)S(1)}, u32[]{:S(2)}, u32[]{:S(2)}) async-start(bf16[128,16,128]{0,2,1:T(8,128)(2,1)} %bitcast.14), calls=%async_computation | async-start | bytes 1048576 | tf_op jit(solution)/shard_map/all_to_all | solution.py:92
  60.6 8.1 %all-to-all-done = bf16[128,16,128]{0,2,1:T(8,128)(2,1)S(1)} async-done(((bf16[128,16,128]{0,2,1:T(8,128)(2,1)}), bf16[128,16,128]{0,2,1:T(8,128)(2,1)S(1)}, u32[]{:S(2)}, u32[]{:S(2)}) %all-to-all-start) | async-done | bytes 524320 | tf_op jit(solution)/shard_map/all_to_all | solution.py:92
  69.0 9.9 %while.10 = (s32[]{:T(128)}, bf16[4,512,128]{2,1,0:T(8,128)(2,1)S(1)}, s32[4,512]{1,0:T(4,128)S(1)}, s32[2048]{0:T(1024)S(1)}, bf16[4,512,1,128]{3,1,2,0:T(8,128...) while((s32[]{:T(128)}, ...), condition=%wide.region_7.8_spmd, body=%wide.region_4.7_spmd.sunk | while | flops 545389568 | bytes 13918305 | solution.py:65
  79.7 4.6 %all-to-all-start.3 = ((bf16[16,128,128]{2,1,0:T(8,128)(2,1)}), bf16[16,128,128]{2,1,0:T(8,128)(2,1)S(1)}, u32[]{:S(2)}, u32[]{:S(2)}) async-start(bf16[16,128,128]{2,1,0:T(8,128)(2,1)} %bitcast.157), calls=%async_computation.3 | async-start | bytes 1048576 | tf_op jit(solution)/shard_map/all_to_all | solution.py:114
  85.0 9.1 %all-to-all-done.3 = bf16[16,128,128]{2,1,0:T(8,128)(2,1)S(1)} async-done(((bf16[16,128,128]{2,1,0:T(8,128)(2,1)}), bf16[16,128,128]{2,1,0:T(8,128)(2,1)S(1)}, u32[]{:S(2)}, u32[]{:S(2)}) %all-to-all-start.3) | async-done | bytes 524320 | tf_op jit(solution)/shard_map/all_to_all | solution.py:114
  96.5 4.9 %all-to-all-start.4 = ((bf16[16,16,4096]{2,1,0:T(8,128)(2,1)}), bf16[16,16,4096]{2,1,0:T(8,128)(2,1)S(1)}, u32[]{:S(2)}, u32[]{:S(2)}) async-start(bf16[16,16,4096]{2,1,0:T(8,128)(2,1)} %bitcast.27), calls=%async_computation.4 | async-start | bytes 4194304 | tf_op jit(solution)/shard_map/all_to_all | solution.py:133
  102.3 26.0 %all-to-all-done.4 = bf16[16,16,4096]{2,1,0:T(8,128)(2,1)S(1)} async-done(((bf16[16,16,4096]{2,1,0:T(8,128)(2,1)}), bf16[16,16,4096]{2,1,0:T(8,128)(2,1)S(1)}, u32[]{:S(2)}, u32[]{:S(2)}) %all-to-all-start.4) | async-done | bytes 2097184 | tf_op jit(solution)/shard_map/all_to_all | solution.py:133
  128.3 2.3 all-gather.6.cloned.1.call-done
  133.1 6.9 %scatter_custom_fusion = bf16[2176,128]{1,0:T(8,128)(2,1)} fusion(s32[2048]{0:T(1024)S(1)} %bitcast.163, bf16[2048,128]{1,0:T(8,128)(2,1)} %bitcast.155, bf16[]{:T(256)} %constant.83.clone.1), kind=kCustom, calls=%fused_computation.51 | custom fusion | bytes 557568 | tf_op jit(solution)/shard_map/scatter | solution.py:103
  139.9 6.5 %scatter_custom_fusion.1 = bf16[2176,128]{1,0:T(8,128)(2,1)} fusion(s32[2048]{0:T(1024)S(1)} %bitcast.164, bf16[2048,128]{1,0:T(8,128)(2,1)S(1)} %bitcast.140, bf16[]{:T(256)} %constant.83.clone.1), kind=kCustom, calls=%fused_computation.49 | custom fusion | bytes 557058 | tf_op jit(solution)/shard_map/scatter | solution.py:109
  146.5 2.2 slice_bitcast_fusion
  152.6 2.3 reshape.265
  156.6 2.5 %reshape_reshape.6 = bf16[2048,256]{1,0:T(8,128)(2,1)} reshape(bf16[32,16384]{1,0:T(8,128)(2,1)} %get-tuple-element.123) | data formatting | bytes 2097152 | tf_op jit(solution)/shard_map/reshape;reshape | solution.py:144
  160.4 49.4 %all-gather.4.cloned.1.call-done = bf16[2048,2048]{1,0:T(8,128)(2,1)} async-done(((bf16[2048,128]{1,0:T(8,128)(2,1)}), bf16[2048,2048]{1,0:T(8,128)(2,1)}) %all-gather.4.cloned.1.call-update) | async-done | bytes 8388624 | tf_op jit(solution)/shard_map/all_gather | solution.py:137
  209.8 6.0 %fusion.35 = (f32[16,16]{1,0:T(8,128)S(1)}, bf16[16,16,2048]{2,1,0:T(8,128)(2,1)S(1)}) fusion(bf16[2048,2048]{1,0:T(8,128)(2,1)} %all-gather.4.cloned.1.call-done, bf16[16,16,4096]{2,1,0:T(8,128)(2,1)S(1)} %copy-done.5), kind=kOutput, calls=%fused_computation.34 | convolution fusion | flops 2150629120 | bytes 11535360 | tf_op jit(solution)/shard_map/...r,cr->...c/dot_general | solution.py:153
  217.7 3.6 %convolution_convert_fusion = bf16[16,16,2048]{2,1,0:T(8,128)(2,1)} fusion(bf16[256,2048]{0,1:T(8,128)(2,1)S(1)} %bitcast.151, bf16[2048,256]{1,0:T(8,128)(2,1)S(1)} %copy-done.8, bf16[16,16,2048]{2,1,0:T(8,128)(2,1)} %copy-done.18, f32[2048]{0:T(1024)S(1)} %copy-done.17, f32[16,16]{1,0:T(8,128)S(1)} %add_rsqrt_fusion, f32[16,16,256]{2,1,0:T(8,128)S(1)} %fusion.42), kind=kOutput, calls=%fused_computation.27 | convolution fusion | flops 539885568 | bytes 4465664 | tf_op jit(solution)/shard_map/smp,pd->smd/dot_general | solution.py:169
  221.3 3.9 %all-to-all-start.5 = ((bf16[16,16,2048]{2,1,0:T(8,128)(2,1)}), bf16[16,16,2048]{2,1,0:T(8,128)(2,1)S(1)}, u32[]{:S(2)}, u32[]{:S(2)}) async-start(bf16[16,16,2048]{2,1,0:T(8,128)(2,1)} %convolution_convert_fusion), calls=%async_computation.5 | async-start | bytes 2097152 | tf_op jit(solution)/shard_map/all_to_all | solution.py:172
  225.3 7.1 %fusion.33 = bf16[128,2048]{1,0:T(8,128)(2,1)} fusion(bf16[128,2048]{1,0:T(8,128)(2,1)S(1)} %copy-done.3, bf16[2048,2048]{1,0:T(8,128)(2,1)} %all-gather.4.cloned.1.call-done, bf16[128,2048]{1,0:T(8,128)(2,1)S(1)} %copy-done.2), kind=kOutput, calls=%fused_computation.30 | convolution fusion | flops 1074528256 | bytes 9961472 | tf_op jit(solution)/shard_map/...r,cr->...c/dot_general | solution.py:153
  232.3 8.3 %all-to-all-done.5 = bf16[16,16,2048]{2,1,0:T(8,128)(2,1)S(1)} async-done(((bf16[16,16,2048]{2,1,0:T(8,128)(2,1)}), bf16[16,16,2048]{2,1,0:T(8,128)(2,1)S(1)}, u32[]{:S(2)}, u32[]{:S(2)}) %all-to-all-start.5) | async-done | bytes 1048608 | tf_op jit(solution)/shard_map/all_to_all | solution.py:172
  (110 shorter events, 37.3 us)
Async XLA Ops:
  7.2 37.4 %copy-start.10 = (bf16[128,2048]{1,0:T(8,128)(2,1)S(1)}, bf16[128,2048]{1,0:T(8,128)(2,1)}, u32[]{:S(2)}) copy-start(bf16[128,2048]{1,0:T(8,128)(2,1)} %param.16) | copy-start | bytes 1572868
  7.2 23.0 %copy-start.9 = (bf16[128,2048]{1,0:T(8,128)(2,1)S(1)}, bf16[128,2048]{1,0:T(8,128)(2,1)}, u32[]{:S(2)}) copy-start(bf16[128,2048]{1,0:T(8,128)(2,1)} %param.18) | copy-start | bytes 1572868
  17.5 42.2 %copy-start.16 = (s32[1,2]{1,0:T(1,128)S(1)}, s32[1,2]{1,0:T(1,128)}, u32[]{:S(2)}) copy-start(s32[1,2]{1,0:T(1,128)} %param.19) | copy-start | bytes 28
  19.6 20.4 %all-to-all-start.1 = ((bf16[128,16,128]{0,2,1:T(8,128)(2,1)}), bf16[128,16,128]{0,2,1:T(8,128)(2,1)S(1)}, u32[]{:S(2)}, u32[]{:S(2)}) async-start(bf16[128,16,128]{0,2,1:T(8,128)(2,1)} %bitcast.18), calls=%async_computation.1 | async-start | bytes 1048576 | tf_op jit(solution)/shard_map/all_to_all | solution.py:93
  40.0 14.4 %all-to-all-start.2 = ((bf16[128,16,128]{0,2,1:T(8,128)(2,1)}), bf16[128,16,128]{0,2,1:T(8,128)(2,1)S(1)}, u32[]{:S(2)}, u32[]{:S(2)}) async-start(bf16[128,16,128]{0,2,1:T(8,128)(2,1)} %bitcast.21), calls=%async_computation.2 | async-start | bytes 1048576 | tf_op jit(solution)/shard_map/all_to_all | solution.py:94
  54.3 14.4 %all-to-all-start = ((bf16[128,16,128]{0,2,1:T(8,128)(2,1)}), bf16[128,16,128]{0,2,1:T(8,128)(2,1)S(1)}, u32[]{:S(2)}, u32[]{:S(2)}) async-start(bf16[128,16,128]{0,2,1:T(8,128)(2,1)} %bitcast.14), calls=%async_computation | async-start | bytes 1048576 | tf_op jit(solution)/shard_map/all_to_all | solution.py:92
  59.0 71.6 %all-gather.6.cloned.1.call-start = ((), (), s32[]{:S(2)}) async-start(), calls=%async_computation.7 | async-start | bytes 3899392 | tf_op jit(solution)/shard_map/all_gather | solution.py:112
  69.0 15.3 %copy-start.13 = (s32[128,8]{0,1:T(8,128)S(1)}, s32[128,8]{0,1:T(8,128)}, u32[]{:S(2)}) copy-start(s32[128,8]{0,1:T(8,128)} %param.26) | copy-start | bytes 12292
  69.0 15.7 %copy-start.1 = (bf16[128,2048]{1,0:T(8,128)(2,1)S(1)}, bf16[128,2048]{1,0:T(8,128)(2,1)}, u32[]{:S(2)}) copy-start(bf16[128,2048]{1,0:T(8,128)(2,1)} %param.15) | copy-start | bytes 1572868
  78.9 5.7 %copy-start.11 = (bf16[2048,1,128]{2,0,1:T(8,128)(2,1)}, bf16[2048,1,128]{2,0,1:T(8,128)(2,1)S(1)}, u32[]{:S(2)}) copy-start(bf16[2048,1,128]{2,0,1:T(8,128)(2,1)S(1)} %get-tuple-element.216) | copy-start | bytes 1572868
  79.7 14.4 %all-to-all-start.3 = ((bf16[16,128,128]{2,1,0:T(8,128)(2,1)}), bf16[16,128,128]{2,1,0:T(8,128)(2,1)S(1)}, u32[]{:S(2)}, u32[]{:S(2)}) async-start(bf16[16,128,128]{2,1,0:T(8,128)(2,1)} %bitcast.157), calls=%async_computation.3 | async-start | bytes 1048576 | tf_op jit(solution)/shard_map/all_to_all | solution.py:114
  96.5 36.4 %copy-start.15 = (s32[1,17]{1,0:T(1,128)S(1)}, s32[1,17]{1,0:T(1,128)}, u32[]{:S(2)}) copy-start(s32[1,17]{1,0:T(1,128)} %param.20) | copy-start | bytes 208
  96.5 31.8 %all-to-all-start.4 = ((bf16[16,16,4096]{2,1,0:T(8,128)(2,1)}), bf16[16,16,4096]{2,1,0:T(8,128)(2,1)S(1)}, u32[]{:S(2)}, u32[]{:S(2)}) async-start(bf16[16,16,4096]{2,1,0:T(8,128)(2,1)} %bitcast.27), calls=%async_computation.4 | async-start | bytes 4194304 | tf_op jit(solution)/shard_map/all_to_all | solution.py:133
  101.4 108.3 %all-gather.4.cloned.1.call-start = ((), (), s32[]{:S(2)}) async-start(), calls=%async_computation.6 | async-start | bytes 8912896 | tf_op jit(solution)/shard_map/all_gather | solution.py:137
  128.3 20.4 %copy-start.4 = (bf16[16,16,4096]{2,1,0:T(8,128)(2,1)}, bf16[16,16,4096]{2,1,0:T(8,128)(2,1)S(1)}, u32[]{:S(2)}) copy-start(bf16[16,16,4096]{2,1,0:T(8,128)(2,1)S(1)} %all-to-all-done.4) | copy-start | bytes 6291460
  154.9 4.2 %copy-start = (bf16[32,16384]{1,0:T(8,128)(2,1)S(1)}, bf16[32,16384]{1,0:T(8,128)(2,1)}, u32[]{:S(2)}) copy-start(bf16[32,16384]{1,0:T(8,128)(2,1)} %get-tuple-element.122) | copy-start | bytes 3145732
  156.6 53.2 %copy-start.5 = (bf16[16,16,4096]{2,1,0:T(8,128)(2,1)S(1)}, bf16[16,16,4096]{2,1,0:T(8,128)(2,1)}, u32[]{:S(2)}) copy-start(bf16[16,16,4096]{2,1,0:T(8,128)(2,1)} %copy-done.4) | copy-start | bytes 6291460
  160.4 56.4 %copy-start.17 = (f32[2048]{0:T(1024)S(1)}, f32[2048]{0:T(1024)}, u32[]{:S(2)}) copy-start(f32[2048]{0:T(1024)} %param.22) | copy-start | bytes 24580
  209.8 7.1 %copy-start.7 = (bf16[2048,256]{1,0:T(8,128)(2,1)S(1)}, bf16[2048,256]{1,0:T(8,128)(2,1)}, u32[]{:S(2)}) copy-start(bf16[2048,256]{1,0:T(8,128)(2,1)} %reshape_reshape.6) | copy-start | bytes 3145732
  215.8 1.9 copy-start.8
  217.7 7.6 %copy-start.14 = (f32[128,8]{0,1:T(8,128)S(1)}, f32[128,8]{0,1:T(8,128)}, u32[]{:S(2)}) copy-start(f32[128,8]{0,1:T(8,128)} %param.27) | copy-start | bytes 12292
  217.7 7.6 %copy-start.2 = (bf16[128,2048]{1,0:T(8,128)(2,1)S(1)}, bf16[128,2048]{1,0:T(8,128)(2,1)}, u32[]{:S(2)}) copy-start(bf16[128,2048]{1,0:T(8,128)(2,1)} %param.15) | copy-start | bytes 1572868
  217.7 7.6 %copy-start.3 = (bf16[128,2048]{1,0:T(8,128)(2,1)S(1)}, bf16[128,2048]{1,0:T(8,128)(2,1)}, u32[]{:S(2)}) copy-start(bf16[128,2048]{1,0:T(8,128)(2,1)} %copy_bitcast_fusion.1) | copy-start | bytes 1572868
  221.3 19.4 %all-to-all-start.5 = ((bf16[16,16,2048]{2,1,0:T(8,128)(2,1)}), bf16[16,16,2048]{2,1,0:T(8,128)(2,1)S(1)}, u32[]{:S(2)}, u32[]{:S(2)}) async-start(bf16[16,16,2048]{2,1,0:T(8,128)(2,1)} %convolution_convert_fusion), calls=%async_computation.5 | async-start | bytes 2097152 | tf_op jit(solution)/shard_map/all_to_all | solution.py:172
  (3 other events, 3.5 us)
Sparse Core Ops, SparseCore 0:
  61.8 68.7 all-gather.5
  133.2 76.4 all-gather.3
